TPU v7x, 128 devices: a whole 4x4x4 slice. The times are simulated.
128 devices in a mesh: blk: 16 (over y, x_hi, core), aux: 8 (over z, x_lo).
Axes of the slice: x: 4 (x_hi: 2, x_lo: 2; x = x_hi * 2 + x_lo), y: 4, z: 4, core: 2. Of those that a mesh axis runs over, the one named last changes fastest.
Arguments:
- three_center: bfloat16 [16, 16, 256, 128, 128], P('blk', None, 'aux'), may hold values from -6 to 6
- slab_factor: bfloat16 [256, 256, 256], P('aux'), may hold values from -0.0234375 to 0.0234375
- coefficients: bfloat16 [8192, 256], P('blk'), may hold values from -0.5 to 0.5
- tile_owner: int32 [16, 16, 1], P('blk'), may hold values from 0 to 15; in each aligned block of 16 rows (0 to 15, 16 to 31, ..., all dimensions but the last counted through in order) at most 2 rows name the same one
- tile_block: int32 [16, 16], P('blk'), may hold values from 0 to 3
- tile_lam: int32 [16, 16], P('blk'), may hold values from 0 to 3
Outputs:
- exchange_slab: float32 [64, 256, 128], P('blk', 'aux')
Inputs may be any that keep to these rules, and one draw needn't show every extreme that they name: `tile_owner`: among the 16 tiles of one blk index at most 2 name the same owner, a bound that some block reaches.
All inputs are finite; a program needn't handle non-finite values.
Results may differ from a plain program's by a relative error of at most 0.0029.
Values may be sent and summed in bfloat16 or wider, within the bound.
No kernel may reach another device: no remote copies, remote signals or barrier semaphores. Data moves between devices by JAX's collectives and lax.ppermute only.
A program may use at most 128 MiB of HBM per device.

v0:
```python
import jax
import jax.numpy as jnp
from jax import lax
from jax.sharding import PartitionSpec as P

CAP = 2


def owned_from(received, labels, blocks_dev):
    flat_tiles = received.reshape((-1,) + received.shape[2:])
    label_ids = labels.reshape(-1).astype(jnp.int32)
    selector = (label_ids[:, None] == jnp.arange(blocks_dev, dtype=jnp.int32)[None, :]).astype(
        jnp.float32
    )
    return jnp.einsum("sk,smc->kmc", selector, flat_tiles, precision=lax.Precision.HIGHEST)


def local(three_center, slab_factor, coefficients, tile_owner, tile_block, tile_lam):
    tile_data = three_center[0]
    cycle_size = lax.axis_size("blk")
    tiles_dev = tile_data.shape[0]
    per_group = tiles_dev // cycle_size
    block_size = tile_data.shape[2]
    rows_dev = coefficients.shape[0]
    blocks_dev = rows_dev // block_size
    occupied = coefficients.shape[1]
    lam_local = tile_lam[0]

    def one_tile(items):
        single_data, panel = items
        half_tile = jnp.einsum(
            "pxl,li->pxi", single_data, panel, preferred_element_type=jnp.float32
        ).astype(jnp.bfloat16)
        return jnp.einsum("pmi,pxi->mx", slab_factor, half_tile, preferred_element_type=jnp.float32)

    panel_rows = lax.all_gather(coefficients, "blk", axis=0, tiled=True)
    groups = panel_rows.shape[0] // rows_dev
    tile_count = groups * per_group
    local_ids = jnp.arange(tile_count, dtype=jnp.int32)
    block_index = local_ids // per_group * blocks_dev + lam_local
    panel_blocks = panel_rows.reshape(groups * blocks_dev, block_size, occupied)
    chosen_panels = panel_blocks[block_index]
    partial_value = lax.map(one_tile, (tile_data, chosen_panels))
    owner_ids = tile_owner[0, :, 0]
    block_ids = tile_block[0]
    same_owner = owner_ids[:, None] == owner_ids[None, :]
    earlier = (
        jnp.arange(tiles_dev, dtype=jnp.int32)[None, :]
        < jnp.arange(tiles_dev, dtype=jnp.int32)[:, None]
    )
    slot_rank = jnp.sum((same_owner & earlier).astype(jnp.int32), axis=1)
    position = owner_ids * CAP + slot_rank
    sending = (jnp.arange(cycle_size * CAP, dtype=jnp.int32)[:, None] == position[None, :]).astype(
        jnp.float32
    )
    labels = jnp.dot(
        sending, block_ids.astype(jnp.float32), precision=lax.Precision.HIGHEST
    ).reshape(cycle_size, CAP)
    send_tiles = jnp.einsum("st,tmc->smc", sending, partial_value, precision=lax.Precision.HIGHEST)
    send_tiles = send_tiles.reshape((cycle_size, CAP) + send_tiles.shape[1:])
    received, got_labels = (
        lax.all_to_all(send_tiles, "blk", split_axis=0, concat_axis=0, tiled=True),
        lax.all_to_all(labels, "blk", split_axis=0, concat_axis=0, tiled=True),
    )
    owned_sum = owned_from(received, got_labels, blocks_dev)
    result = lax.psum_scatter(owned_sum, "aux", scatter_dimension=1, tiled=True)
    return result


def solution(mesh):
    placed = (
        P("blk", None, "aux", None, None),
        P("aux", None, None),
        P("blk", None),
        P("blk", None, None),
        P("blk", None),
        P("blk", None),
    )
    return jax.shard_map(
        local, mesh=mesh, in_specs=placed, out_specs=P("blk", "aux", None), check_vma=False
    )
```

profile of v0, /device:TPU:1, one launch (start us, length us, event | category | flops | bytes accessed | tf_op | source)
XLA Modules:
  0.0 339.3 jit_solution(14537251614347780838)
XLA Ops:
  6.5 0.7 all-gather.2.cloned.1.call-update
  7.3 0.9 convert_reduce_fusion.1
  8.9 0.8 fusion.17
  9.7 0.8 copy.18
  10.5 8.4 %all-to-all-start = ((f32[16,1,2]{2,1,0:T(1,128)}), f32[16,1,2]{2,1,0:T(1,128)S(1)}, u32[]{:S(2)}, u32[]{:S(2)}) async-start(f32[16,1,2]{2,1,0:T(1,128)} %copy.18), calls=%async_computation | async-start | bytes 16384 | tf_op jit(solution)/shard_map/all_to_all | solution.py:63
  19.6 48.6 %all-gather.2.cloned.1.call-done = bf16[8192,256]{1,0:T(8,128)(2,1)} async-done(((bf16[512,256]{1,0:T(8,128)(2,1)}), bf16[8192,256]{1,0:T(8,128)(2,1)}) %all-gather.2.cloned.1.call-update) | async-done | bytes 4194320 | tf_op jit(solution)/shard_map/all_gather | solution.py:36
  68.2 2.8 gather_fusion
  71.0 122.3 %while.10 = (s32[]{:T(128)}, f32[16,256,128]{2,0,1:T(8,128)S(1)}, bf16[16,32,128,128]{3,2,1,0:T(8,128)(2,1)}, bf16[16,128,256]{2,1,0:T(8,128)(2,1)S(1)}, bf16[32...) while((s32[]{:T(128)}, f32[16,256,128]{2,0,1:T(8,128)S(1)}, bf16[16,32,128,128]{3,2,1,0:T(8,128)(2,1)}, ...), condition=%wide.region_2.3_spmd, body=%wide.region_1.2_spmd.sunk | while | flops 806354944 | bytes 5964881 | solution.py:43
  71.0 4.7 %fusion.41 = f32[1,256,128]{1,2,0:T(8,128)S(1)} fusion(bf16[32,256,256]{2,1,0:T(8,128)(2,1)} %get-tuple-element.92, bf16[16,32,128,128]{3,2,1,0:T(8,128)(2,1)} %get-tuple-element.90, s32[]{:T(128)} %get-tuple-element.81, bf16[16,128,256]{2,1,0:T(8,128)(2,1)S(1)} %get-tuple-element.91), kind=kOutput, calls=%fused_computation.4.clone.1 | convolution fusion | flops 806354944 | bytes 5440512 | tf_op jit(solution)/shard_map/while/body/eval_jaxpr/pmi,pxi->mx/dot_general | solution.py:34
  75.8 2.8 dynamic_update_slice.5
  78.6 4.7 %fusion.41 = f32[1,256,128]{1,2,0:T(8,128)S(1)} fusion(bf16[32,256,256]{2,1,0:T(8,128)(2,1)} %get-tuple-element.92, bf16[16,32,128,128]{3,2,1,0:T(8,128)(2,1)} %get-tuple-element.90, s32[]{:T(128)} %get-tuple-element.81, bf16[16,128,256]{2,1,0:T(8,128)(2,1)S(1)} %get-tuple-element.91), kind=kOutput, calls=%fused_computation.4.clone.1 | convolution fusion | flops 806354944 | bytes 5440512 | tf_op jit(solution)/shard_map/while/body/eval_jaxpr/pmi,pxi->mx/dot_general | solution.py:34
  83.4 2.8 dynamic_update_slice.5
  86.3 4.7 %fusion.41 = f32[1,256,128]{1,2,0:T(8,128)S(1)} fusion(bf16[32,256,256]{2,1,0:T(8,128)(2,1)} %get-tuple-element.92, bf16[16,32,128,128]{3,2,1,0:T(8,128)(2,1)} %get-tuple-element.90, s32[]{:T(128)} %get-tuple-element.81, bf16[16,128,256]{2,1,0:T(8,128)(2,1)S(1)} %get-tuple-element.91), kind=kOutput, calls=%fused_computation.4.clone.1 | convolution fusion | flops 806354944 | bytes 5440512 | tf_op jit(solution)/shard_map/while/body/eval_jaxpr/pmi,pxi->mx/dot_general | solution.py:34
  91.0 2.8 dynamic_update_slice.5
  93.9 4.7 %fusion.41 = f32[1,256,128]{1,2,0:T(8,128)S(1)} fusion(bf16[32,256,256]{2,1,0:T(8,128)(2,1)} %get-tuple-element.92, bf16[16,32,128,128]{3,2,1,0:T(8,128)(2,1)} %get-tuple-element.90, s32[]{:T(128)} %get-tuple-element.81, bf16[16,128,256]{2,1,0:T(8,128)(2,1)S(1)} %get-tuple-element.91), kind=kOutput, calls=%fused_computation.4.clone.1 | convolution fusion | flops 806354944 | bytes 5440512 | tf_op jit(solution)/shard_map/while/body/eval_jaxpr/pmi,pxi->mx/dot_general | solution.py:34
  98.7 2.8 dynamic_update_slice.5
  101.5 4.7 %fusion.41 = f32[1,256,128]{1,2,0:T(8,128)S(1)} fusion(bf16[32,256,256]{2,1,0:T(8,128)(2,1)} %get-tuple-element.92, bf16[16,32,128,128]{3,2,1,0:T(8,128)(2,1)} %get-tuple-element.90, s32[]{:T(128)} %get-tuple-element.81, bf16[16,128,256]{2,1,0:T(8,128)(2,1)S(1)} %get-tuple-element.91), kind=kOutput, calls=%fused_computation.4.clone.1 | convolution fusion | flops 806354944 | bytes 5440512 | tf_op jit(solution)/shard_map/while/body/eval_jaxpr/pmi,pxi->mx/dot_general | solution.py:34
  106.3 2.8 dynamic_update_slice.5
  109.2 4.7 %fusion.41 = f32[1,256,128]{1,2,0:T(8,128)S(1)} fusion(bf16[32,256,256]{2,1,0:T(8,128)(2,1)} %get-tuple-element.92, bf16[16,32,128,128]{3,2,1,0:T(8,128)(2,1)} %get-tuple-element.90, s32[]{:T(128)} %get-tuple-element.81, bf16[16,128,256]{2,1,0:T(8,128)(2,1)S(1)} %get-tuple-element.91), kind=kOutput, calls=%fused_computation.4.clone.1 | convolution fusion | flops 806354944 | bytes 5440512 | tf_op jit(solution)/shard_map/while/body/eval_jaxpr/pmi,pxi->mx/dot_general | solution.py:34
  114.0 2.8 dynamic_update_slice.5
  116.8 4.7 %fusion.41 = f32[1,256,128]{1,2,0:T(8,128)S(1)} fusion(bf16[32,256,256]{2,1,0:T(8,128)(2,1)} %get-tuple-element.92, bf16[16,32,128,128]{3,2,1,0:T(8,128)(2,1)} %get-tuple-element.90, s32[]{:T(128)} %get-tuple-element.81, bf16[16,128,256]{2,1,0:T(8,128)(2,1)S(1)} %get-tuple-element.91), kind=kOutput, calls=%fused_computation.4.clone.1 | convolution fusion | flops 806354944 | bytes 5440512 | tf_op jit(solution)/shard_map/while/body/eval_jaxpr/pmi,pxi->mx/dot_general | solution.py:34
  121.6 2.8 dynamic_update_slice.5
  124.5 4.7 %fusion.41 = f32[1,256,128]{1,2,0:T(8,128)S(1)} fusion(bf16[32,256,256]{2,1,0:T(8,128)(2,1)} %get-tuple-element.92, bf16[16,32,128,128]{3,2,1,0:T(8,128)(2,1)} %get-tuple-element.90, s32[]{:T(128)} %get-tuple-element.81, bf16[16,128,256]{2,1,0:T(8,128)(2,1)S(1)} %get-tuple-element.91), kind=kOutput, calls=%fused_computation.4.clone.1 | convolution fusion | flops 806354944 | bytes 5440512 | tf_op jit(solution)/shard_map/while/body/eval_jaxpr/pmi,pxi->mx/dot_general | solution.py:34
  129.2 2.8 dynamic_update_slice.5
  132.1 4.7 %fusion.41 = f32[1,256,128]{1,2,0:T(8,128)S(1)} fusion(bf16[32,256,256]{2,1,0:T(8,128)(2,1)} %get-tuple-element.92, bf16[16,32,128,128]{3,2,1,0:T(8,128)(2,1)} %get-tuple-element.90, s32[]{:T(128)} %get-tuple-element.81, bf16[16,128,256]{2,1,0:T(8,128)(2,1)S(1)} %get-tuple-element.91), kind=kOutput, calls=%fused_computation.4.clone.1 | convolution fusion | flops 806354944 | bytes 5440512 | tf_op jit(solution)/shard_map/while/body/eval_jaxpr/pmi,pxi->mx/dot_general | solution.py:34
  136.9 2.8 dynamic_update_slice.5
  139.8 4.7 %fusion.41 = f32[1,256,128]{1,2,0:T(8,128)S(1)} fusion(bf16[32,256,256]{2,1,0:T(8,128)(2,1)} %get-tuple-element.92, bf16[16,32,128,128]{3,2,1,0:T(8,128)(2,1)} %get-tuple-element.90, s32[]{:T(128)} %get-tuple-element.81, bf16[16,128,256]{2,1,0:T(8,128)(2,1)S(1)} %get-tuple-element.91), kind=kOutput, calls=%fused_computation.4.clone.1 | convolution fusion | flops 806354944 | bytes 5440512 | tf_op jit(solution)/shard_map/while/body/eval_jaxpr/pmi,pxi->mx/dot_general | solution.py:34
  144.5 2.8 dynamic_update_slice.5
  147.4 4.7 %fusion.41 = f32[1,256,128]{1,2,0:T(8,128)S(1)} fusion(bf16[32,256,256]{2,1,0:T(8,128)(2,1)} %get-tuple-element.92, bf16[16,32,128,128]{3,2,1,0:T(8,128)(2,1)} %get-tuple-element.90, s32[]{:T(128)} %get-tuple-element.81, bf16[16,128,256]{2,1,0:T(8,128)(2,1)S(1)} %get-tuple-element.91), kind=kOutput, calls=%fused_computation.4.clone.1 | convolution fusion | flops 806354944 | bytes 5440512 | tf_op jit(solution)/shard_map/while/body/eval_jaxpr/pmi,pxi->mx/dot_general | solution.py:34
  152.2 2.8 dynamic_update_slice.5
  155.0 4.7 %fusion.41 = f32[1,256,128]{1,2,0:T(8,128)S(1)} fusion(bf16[32,256,256]{2,1,0:T(8,128)(2,1)} %get-tuple-element.92, bf16[16,32,128,128]{3,2,1,0:T(8,128)(2,1)} %get-tuple-element.90, s32[]{:T(128)} %get-tuple-element.81, bf16[16,128,256]{2,1,0:T(8,128)(2,1)S(1)} %get-tuple-element.91), kind=kOutput, calls=%fused_computation.4.clone.1 | convolution fusion | flops 806354944 | bytes 5440512 | tf_op jit(solution)/shard_map/while/body/eval_jaxpr/pmi,pxi->mx/dot_general | solution.py:34
  159.8 2.8 dynamic_update_slice.5
  162.7 4.7 %fusion.41 = f32[1,256,128]{1,2,0:T(8,128)S(1)} fusion(bf16[32,256,256]{2,1,0:T(8,128)(2,1)} %get-tuple-element.92, bf16[16,32,128,128]{3,2,1,0:T(8,128)(2,1)} %get-tuple-element.90, s32[]{:T(128)} %get-tuple-element.81, bf16[16,128,256]{2,1,0:T(8,128)(2,1)S(1)} %get-tuple-element.91), kind=kOutput, calls=%fused_computation.4.clone.1 | convolution fusion | flops 806354944 | bytes 5440512 | tf_op jit(solution)/shard_map/while/body/eval_jaxpr/pmi,pxi->mx/dot_general | solution.py:34
  167.5 2.8 dynamic_update_slice.5
  170.3 4.7 %fusion.41 = f32[1,256,128]{1,2,0:T(8,128)S(1)} fusion(bf16[32,256,256]{2,1,0:T(8,128)(2,1)} %get-tuple-element.92, bf16[16,32,128,128]{3,2,1,0:T(8,128)(2,1)} %get-tuple-element.90, s32[]{:T(128)} %get-tuple-element.81, bf16[16,128,256]{2,1,0:T(8,128)(2,1)S(1)} %get-tuple-element.91), kind=kOutput, calls=%fused_computation.4.clone.1 | convolution fusion | flops 806354944 | bytes 5440512 | tf_op jit(solution)/shard_map/while/body/eval_jaxpr/pmi,pxi->mx/dot_general | solution.py:34
  175.1 2.8 dynamic_update_slice.5
  178.0 4.7 %fusion.41 = f32[1,256,128]{1,2,0:T(8,128)S(1)} fusion(bf16[32,256,256]{2,1,0:T(8,128)(2,1)} %get-tuple-element.92, bf16[16,32,128,128]{3,2,1,0:T(8,128)(2,1)} %get-tuple-element.90, s32[]{:T(128)} %get-tuple-element.81, bf16[16,128,256]{2,1,0:T(8,128)(2,1)S(1)} %get-tuple-element.91), kind=kOutput, calls=%fused_computation.4.clone.1 | convolution fusion | flops 806354944 | bytes 5440512 | tf_op jit(solution)/shard_map/while/body/eval_jaxpr/pmi,pxi->mx/dot_general | solution.py:34
  182.7 2.8 dynamic_update_slice.5
  185.6 4.7 %fusion.41 = f32[1,256,128]{1,2,0:T(8,128)S(1)} fusion(bf16[32,256,256]{2,1,0:T(8,128)(2,1)} %get-tuple-element.92, bf16[16,32,128,128]{3,2,1,0:T(8,128)(2,1)} %get-tuple-element.90, s32[]{:T(128)} %get-tuple-element.81, bf16[16,128,256]{2,1,0:T(8,128)(2,1)S(1)} %get-tuple-element.91), kind=kOutput, calls=%fused_computation.4.clone.1 | convolution fusion | flops 806354944 | bytes 5440512 | tf_op jit(solution)/shard_map/while/body/eval_jaxpr/pmi,pxi->mx/dot_general | solution.py:34
  190.4 2.8 dynamic_update_slice.5
  193.2 2.0 fusion.21
  195.2 4.1 %copy.20 = f32[16,2,256,128]{3,1,2,0:T(2,128)} copy(f32[16,2,256,128]{3,1,0,2:T(2,128)S(1)} %bitcast.54) | data formatting | bytes 8388608 | tf_op jit(solution)/shard_map/reshape | solution.py:60
  199.4 4.5 %all-to-all-start.1 = ((f32[16,2,256,128]{3,1,2,0:T(2,128)}), f32[16,2,256,128]{3,1,2,0:T(2,128)}, u32[]{:S(2)}, u32[]{:S(2)}) async-start(f32[16,2,256,128]{3,1,2,0:T(2,128)} %copy.20), calls=%async_computation.1 | async-start | bytes 8388608 | tf_op jit(solution)/shard_map/all_to_all | solution.py:62
  204.0 50.8 %all-to-all-done.1 = f32[16,2,256,128]{3,1,2,0:T(2,128)} async-done(((f32[16,2,256,128]{3,1,2,0:T(2,128)}), f32[16,2,256,128]{3,1,2,0:T(2,128)}, u32[]{:S(2)}, u32[]{:S(2)}) %all-to-all-start.1) | async-done | bytes 4194336 | tf_op jit(solution)/shard_map/all_to_all | solution.py:62
  254.9 4.6 %copy.21 = f32[16,2,256,128]{3,1,0,2:T(2,128)S(1)} copy(f32[16,2,256,128]{3,1,2,0:T(2,128)} %all-to-all-done.1) | data formatting | bytes 8388608 | tf_op jit(solution)/shard_map/all_to_all | solution.py:62
  259.5 2.3 fusion.25
  263.1 67.9 %all-reduce.3.cloned.1.call-done = f32[4,256,128]{2,0,1:T(4,128)} async-done(((f32[4,256,128]{2,0,1:T(4,128)}), f32[4,256,128]{2,0,1:T(4,128)}) %all-reduce.3.cloned.1.call-update) | async-done | bytes 524304
  331.0 0.8 constant_dynamic-slice_fusion
  (32 shorter events, 4.2 us)
Async XLA Ops:
  6.5 61.6 %all-gather.2.cloned.1.call-start = ((), (), s32[]{:S(2)}) async-start(), calls=%async_computation.2 | async-start | bytes 4456448 | tf_op jit(solution)/shard_map/all_gather | solution.py:36
  10.5 188.9 %all-to-all-start = ((f32[16,1,2]{2,1,0:T(1,128)}), f32[16,1,2]{2,1,0:T(1,128)S(1)}, u32[]{:S(2)}, u32[]{:S(2)}) async-start(f32[16,1,2]{2,1,0:T(1,128)} %copy.18), calls=%async_computation | async-start | bytes 16384 | tf_op jit(solution)/shard_map/all_to_all | solution.py:63
  199.4 55.5 %all-to-all-start.1 = ((f32[16,2,256,128]{3,1,2,0:T(2,128)}), f32[16,2,256,128]{3,1,2,0:T(2,128)}, u32[]{:S(2)}, u32[]{:S(2)}) async-start(f32[16,2,256,128]{3,1,2,0:T(2,128)} %copy.20), calls=%async_computation.1 | async-start | bytes 8388608 | tf_op jit(solution)/shard_map/all_to_all | solution.py:62
  203.9 127.1 %all-reduce.3.cloned.1.call-start = ((), (), s32[]{:S(2)}) async-start(), calls=%async_computation.3 | async-start | bytes 1048576
  259.5 2.3 copy-start
Sparse Core Ops, SparseCore 0:
  9.8 58.3 all-gather.1
  261.9 68.9 all-reduce.2
where the time goes:
time: 344 us; the launch traced here: 339 us
  waiting for transfers between devices  168 us (49%)
  matrix products  79.8 us (23%)
  local copies, waits for them, and re-layouts  61.4 us (18%)
  between operations  14.1 us (4%)
  starting transfers between devices  13 us (4%)
    dot_general x16, matrix products, one_tile(): jnp.einsum('pmi,pxi->mx', slab_factor, half_tile, preferred_element_type=...  74.8 us
    unnamed x3, waiting for transfers between devices  68.6 us
    all_to_all x1, waiting for transfers between devices, local(): lax.all_to_all(send_tiles, 'blk', split_axis=0, concat_axis=0, tiled=True)  50.8 us
    all_gather x1, waiting for transfers between devices, local(): panel_rows = lax.all_gather(coefficients, 'blk', axis=0, tiled=True)  48.6 us
    dynamic_update_slice x32, local copies, waits for them, and re-layouts, local(): partial_value = lax.map(one_tile, (tile_data, chosen_panels))  46.9 us
    all_to_all x1, starting transfers between devices, local(): lax.all_to_all(labels, 'blk', split_axis=0, concat_axis=0, tiled=True)  8.44 us
  transfers between devices with their start and end apart: 4, of which 3 were waited for; matrix products, arithmetic and copies ran while one was open for 40% of the time, Pallas kernels for 0%

commit v1 on v0

v1 whole, which is shorter than its diff:
```python
import functools

import jax
import jax.numpy as jnp
from jax import lax
from jax.experimental import pallas as pl
from jax.experimental.pallas import tpu as pltpu
from jax.sharding import PartitionSpec as P

CAP = 2
P_CHUNK = 8


def tile_kernel(t_ref, c_ref, s_ref, o_ref):
    n_p, bs, _ = t_ref.shape
    panel = c_ref[...]
    acc = None
    for c0 in range(0, n_p, P_CHUNK):
        block = t_ref[c0:c0 + P_CHUNK].reshape(P_CHUNK * bs, bs)
        half = jnp.dot(block, panel, preferred_element_type=jnp.float32).astype(jnp.bfloat16)
        for j in range(P_CHUNK):
            term = lax.dot_general(
                s_ref[c0 + j],
                half[j * bs:(j + 1) * bs],
                (((1,), (1,)), ((), ())),
                preferred_element_type=jnp.float32,
            )
            acc = term if acc is None else acc + term
    o_ref[...] = acc.reshape(o_ref.shape)


def tile_partials(tile_data, panels, slab_factor, n_aux):
    tiles, n_p, bs, _ = tile_data.shape
    occ = panels.shape[2]
    slab = slab_factor.shape[1]
    rows = slab // n_aux
    flops = tiles * (2 * n_p * bs * bs * occ + 2 * n_p * slab * occ * bs)
    bytes_accessed = tile_data.size * 2 + panels.size * 2 + slab_factor.size * 2 + tiles * slab * bs * 4
    return pl.pallas_call(
        tile_kernel,
        grid=(tiles,),
        in_specs=[
            pl.BlockSpec((None, n_p, bs, bs), lambda t: (t, 0, 0, 0)),
            pl.BlockSpec((None, bs, occ), lambda t: (t, 0, 0)),
            pl.BlockSpec((n_p, slab, occ), lambda t: (0, 0, 0)),
        ],
        out_specs=pl.BlockSpec((n_aux, None, rows, bs), lambda t: (0, t, 0, 0)),
        out_shape=jax.ShapeDtypeStruct((n_aux, tiles, rows, bs), jnp.float32),
        cost_estimate=pl.CostEstimate(flops=flops, transcendentals=0, bytes_accessed=bytes_accessed),
    )(tile_data, panels, slab_factor)


def local(three_center, slab_factor, coefficients, tile_owner, tile_block, tile_lam):
    tile_data = three_center[0]
    n_blk = lax.axis_size("blk")
    n_aux = lax.axis_size("aux")
    tiles = tile_data.shape[0]
    per_group = tiles // n_blk
    bs = tile_data.shape[2]
    rows_dev, occ = coefficients.shape
    blocks_dev = rows_dev // bs

    owner_ids = tile_owner[0, :, 0]
    block_ids = tile_block[0]
    lam_ids = tile_lam[0]

    same_owner = owner_ids[:, None] == owner_ids[None, :]
    earlier = jnp.arange(tiles)[None, :] < jnp.arange(tiles)[:, None]
    slot_rank = jnp.sum((same_owner & earlier).astype(jnp.int32), axis=1)
    position = owner_ids * CAP + slot_rank
    slot_hit = jnp.arange(n_blk * CAP, dtype=jnp.int32)[:, None] == position[None, :]
    slot_valid = jnp.any(slot_hit, axis=1)
    slot_tile = jnp.sum(jnp.where(slot_hit, jnp.arange(tiles, dtype=jnp.int32)[None, :], 0), axis=1)
    slot_label = jnp.where(slot_valid, block_ids[slot_tile], -1)

    ints = jnp.concatenate(
        [lam_ids.reshape(n_blk, per_group), slot_label.reshape(n_blk, CAP)], axis=1
    ).astype(jnp.int32)
    ints_got = lax.all_to_all(ints, "blk", 0, 0, tiled=True)
    lam_req = ints_got[:, :per_group]
    got_labels = ints_got[:, per_group:]

    coef_blocks = coefficients.reshape(blocks_dev, bs, occ)
    send_panels = coef_blocks[lam_req.reshape(-1)].reshape(n_blk, per_group, bs, occ)
    panels = lax.all_to_all(send_panels, "blk", 0, 0, tiled=True).reshape(tiles, bs, occ)

    partial = tile_partials(tile_data, panels, slab_factor, n_aux)
    reduced = lax.psum_scatter(partial, "aux", scatter_dimension=0, tiled=True)[0]

    picked = reduced[slot_tile]
    send_tiles = jnp.where(slot_valid[:, None, None], picked, 0.0)
    send_tiles = send_tiles.reshape((n_blk, CAP) + send_tiles.shape[1:])
    received = lax.all_to_all(send_tiles, "blk", 0, 0, tiled=True)
    received = received.reshape((n_blk * CAP,) + received.shape[2:])
    labels = got_labels.reshape(-1)
    owned = jnp.stack(
        [jnp.sum(jnp.where((labels == b)[:, None, None], received, 0.0), axis=0) for b in range(blocks_dev)]
    )
    return owned


def solution(mesh):
    placed = (
        P("blk", None, "aux", None, None),
        P("aux", None, None),
        P("blk", None),
        P("blk", None, None),
        P("blk", None),
        P("blk", None),
    )
    return jax.shard_map(
        local, mesh=mesh, in_specs=placed, out_specs=P("blk", "aux", None), check_vma=False
    )
```

time: 344 us -> 174 us (0.51); the launches traced: 339 us -> 174 us
  waiting for transfers between devices: 168 us -> 61.6 us
  matrix products: 79.8 us -> 0 us
  local copies, waits for them, and re-layouts: 61.4 us -> 4.32 us
  Pallas kernels: 0 us -> 47.1 us
  blocking collectives: 0 us -> 35.9 us
  starting transfers between devices: 13 us -> 7.48 us
    dot_general x19 -> x0, matrix products: 79.8 us -> none  [the longest x16 74.8 us: one_tile(): jnp.einsum('pmi,pxi->mx', slab_factor, half_tile, preferred_element_type=...]
    unnamed x3 -> x1, waiting for transfers between devices: 68.6 us -> 0.02 us
    reduce_scatter x0 -> x1, waiting for transfers between devices: none -> 50.8 us  [local(): lax.psum_scatter(partial, 'aux', scatter_dimension=0, tiled=True)[0]]
    all_gather x1 -> x0, waiting for transfers between devices: 48.6 us -> none  [local(): panel_rows = lax.all_gather(coefficients, 'blk', axis=0, tiled=True)]
    pallas_call x0 -> x1, Pallas kernels: none -> 47.1 us  [tile_partials(): pl.pallas_call(tile_kernel, grid=(tiles,), in_specs=[pl.BlockSpec((None,...]
    dynamic_update_slice x32 -> x0, local copies, waits for them, and re-layouts: 46.9 us -> none  [local(): partial_value = lax.map(one_tile, (tile_data, chosen_panels))]
    all_to_all x2 -> x1, waiting for transfers between devices: 50.8 us -> 10.8 us  [local(): received = lax.all_to_all(send_tiles, 'blk', 0, 0, tiled=True)]
    all_to_all x0 -> x2, blocking collectives: none -> 35.9 us  [the longest x1 20.7 us: local(): lax.all_to_all(send_panels, 'blk', 0, 0, tiled=True).reshape(tiles, bs, occ)]
  transfers between devices with their start and end apart: 4 -> 2, of which waited for: 3 -> 2; matrix products, arithmetic and copies ran while one was open for 40% -> 0% of each run, Pallas kernels for 0% -> 0%
where the time goes in v1:
time: 174 us
  waiting for transfers between devices  61.6 us (35%)
  Pallas kernels  47.1 us (27%)
  blocking collectives  35.9 us (21%)
  between operations  13.5 us (8%)
  starting transfers between devices  7.48 us (4%)
  local copies, waits for them, and re-layouts  4.32 us (2%)
  other arithmetic  4.22 us (2%)
    reduce_scatter x1, waiting for transfers between devices, local(): lax.psum_scatter(partial, 'aux', scatter_dimension=0, tiled=True)[0]  50.8 us
    pallas_call x1, Pallas kernels, tile_partials(): pl.pallas_call(tile_kernel, grid=(tiles,), in_specs=[pl.BlockSpec((None,...  47.1 us
    all_to_all x1, blocking collectives, local(): lax.all_to_all(send_panels, 'blk', 0, 0, tiled=True).reshape(tiles, bs, occ)  20.7 us
    all_to_all x1, blocking collectives, local(): ints_got = lax.all_to_all(ints, 'blk', 0, 0, tiled=True)  15.2 us
    all_to_all x1, waiting for transfers between devices, local(): received = lax.all_to_all(send_tiles, 'blk', 0, 0, tiled=True)  10.8 us
    all_to_all x1, starting transfers between devices, local(): received = lax.all_to_all(send_tiles, 'blk', 0, 0, tiled=True)  7.48 us
  transfers between devices with their start and end apart: 2, of which 2 were waited for; matrix products, arithmetic and copies ran while one was open for 0% of the time, Pallas kernels for 0%

profile of v1, /device:TPU:1, one launch (start us, length us, event | category | flops | bytes accessed | tf_op | source)
XLA Modules:
  0.0 174.1 jit_solution(13674096226096023045)
XLA Ops:
  6.5 0.0 copy-start
  6.5 0.0 reduce-scatter.2.cloned.1.call-start
  6.5 0.9 convert_reduce_fusion
  7.5 0.7 multiply_add_fusion
  8.1 0.1 select_reduce_fusion.4
  8.2 0.1 fusion
  8.3 1.4 gather_fusion
  9.7 0.1 gather.14
  9.8 0.1 reduce_or.12
  9.9 0.1 copy.26
  10.0 0.7 add_bitcast_fusion
  10.6 0.1 copy.27
  10.7 15.2 %all_to_all.22 = s32[16,1,3]{2,1,0:T(1,128)S(1)} all-to-all(s32[16,1,3]{2,1,0:T(1,128)S(1)} %copy.27), channel_id=1, replica_groups=mesh['blk'=16,'aux'=8] {'blk'}, dimensions={0} | all-to-all | bytes 384 | tf_op jit(solution)/shard_map/all_to_all | solution.py:79
  25.9 0.1 copy.28
  26.0 0.0 copy-done
  26.0 0.6 gather_fusion.1
  26.7 20.7 %all_to_all.23 = bf16[16,1,128,256]{3,2,1,0:T(8,128)(2,1)} all-to-all(bf16[16,1,128,256]{3,2,1,0:T(8,128)(2,1)S(1)} %bitcast.25), channel_id=1, replica_groups=mesh['blk'=16,'aux'=8] {'blk'}, dimensions={0} | all-to-all | bytes 2097152 | tf_op jit(solution)/shard_map/all_to_all | solution.py:85
  47.3 47.1 %shard_map.64 = f32[8,16,32,128]{3,2,1,0:T(8,128)} custom-call(bf16[16,32,128,128]{3,2,1,0:T(8,128)(2,1)} %bitcast.36, bf16[16,128,256]{2,1,0:T(8,128)(2,1)} %bitcast.27, bf16[32,256,256]{2,1,0:T(8,128)(2,1)} %s_ref.1), custom_call_target="tpu_custom_call" | custom-call | flops 12884901888 | bytes 24117248 | tf_op jit(solution)/shard_map/pallas_call | solution.py:39
  94.5 0.0 reduce-scatter.2.cloned.1.call-update
  94.5 50.8 %reduce-scatter.2.cloned.1.call-done = f32[1,16,32,128]{3,2,1,0:T(8,128)} async-done(((f32[8,16,32,128]{3,2,1,0:T(8,128)}), f32[1,16,32,128]{3,2,1,0:T(8,128)}) %reduce-scatter.2.cloned.1.call-update) | async-done | bytes 262160 | tf_op jit(solution)/shard_map/reduce_scatter | solution.py:88
  145.3 1.5 gather_fusion.2
  146.8 0.9 broadcast_select_fusion
  147.7 7.5 %all-to-all-start.2 = ((f32[16,2,32,128]{3,2,1,0:T(8,128)}), f32[16,2,32,128]{3,2,1,0:T(8,128)S(1)}, u32[]{:S(2)}, u32[]{:S(2)}) async-start(f32[16,2,32,128]{3,2,1,0:T(8,128)} %broadcast_select_fusion), calls=%async_computation.3 | async-start | bytes 1048576 | tf_op jit(solution)/shard_map/all_to_all | solution.py:93
  155.2 0.1 copy.29
  155.3 0.1 copy.30
  155.4 0.1 copy.31
  155.5 0.1 copy.32
  155.6 10.8 %all-to-all-done.2 = f32[16,2,32,128]{3,2,1,0:T(8,128)S(1)} async-done(((f32[16,2,32,128]{3,2,1,0:T(8,128)}), f32[16,2,32,128]{3,2,1,0:T(8,128)S(1)}, u32[]{:S(2)}, u32[]{:S(2)}) %all-to-all-start.2) | async-done | bytes 524320 | tf_op jit(solution)/shard_map/all_to_all | solution.py:93
  166.4 0.2 select_reduce_fusion.3
  166.6 0.6 pad_maximum_fusion
  (6 shorter events, 0.0 us)
Async XLA Ops:
  6.5 19.5 %copy-start = (bf16[512,256]{1,0:T(8,128)(2,1)S(1)}, bf16[512,256]{1,0:T(8,128)(2,1)}, u32[]{:S(2)}) copy-start(bf16[512,256]{1,0:T(8,128)(2,1)} %param.8) | copy-start | bytes 786436
  6.5 138.7 %reduce-scatter.2.cloned.1.call-start = ((), (), s32[]{:S(2)}) async-start(), calls=%async_computation.4 | async-start | bytes 2359296 | tf_op jit(solution)/shard_map/reduce_scatter | solution.py:88
  147.7 18.6 %all-to-all-start.2 = ((f32[16,2,32,128]{3,2,1,0:T(8,128)}), f32[16,2,32,128]{3,2,1,0:T(8,128)S(1)}, u32[]{:S(2)}, u32[]{:S(2)}) async-start(f32[16,2,32,128]{3,2,1,0:T(8,128)} %broadcast_select_fusion), calls=%async_computation.3 | async-start | bytes 1048576 | tf_op jit(solution)/shard_map/all_to_all | solution.py:93
Sparse Core Ops, SparseCore 0:
  94.6 50.6 reduce-scatter.1

commit v2 on v1

--- a/solution.py
+++ b/solution.py
@@ -8,46 +8,59 @@
 from jax.sharding import PartitionSpec as P
 
 CAP = 2
-P_CHUNK = 8
+P_CHUNK = 4
+ROW_CHUNK = 512
 
 
-def tile_kernel(t_ref, c_ref, s_ref, o_ref):
-    n_p, bs, _ = t_ref.shape
-    panel = c_ref[...]
-    acc = None
-    for c0 in range(0, n_p, P_CHUNK):
-        block = t_ref[c0:c0 + P_CHUNK].reshape(P_CHUNK * bs, bs)
-        half = jnp.dot(block, panel, preferred_element_type=jnp.float32).astype(jnp.bfloat16)
-        for j in range(P_CHUNK):
-            term = lax.dot_general(
-                s_ref[c0 + j],
-                half[j * bs:(j + 1) * bs],
-                (((1,), (1,)), ((), ())),
-                preferred_element_type=jnp.float32,
-            )
-            acc = term if acc is None else acc + term
-    o_ref[...] = acc.reshape(o_ref.shape)
+def tile_kernel(t_ref, c_ref, s_ref, o_ref, hbuf, acc):
+    step = pl.program_id(0)
+    tiles, n_p, bs, _ = t_ref.shape
+    occ = c_ref.shape[2]
+
+    @pl.when(step == 0)
+    def _():
+        acc[...] = jnp.zeros_like(acc)
+
+    for t in range(tiles):
+        block = t_ref[t].reshape(n_p * bs, bs)
+        half = jnp.dot(block, c_ref[t], preferred_element_type=jnp.float32).astype(jnp.bfloat16)
+        for j in range(n_p):
+            hbuf[t * bs:(t + 1) * bs, j * occ:(j + 1) * occ] = half[j * bs:(j + 1) * bs]
+    for r in range(0, tiles * bs, ROW_CHUNK):
+        acc[r:r + ROW_CHUNK] += jnp.dot(
+            hbuf[r:r + ROW_CHUNK], s_ref[...], preferred_element_type=jnp.float32
+        )
+
+    @pl.when(step == pl.num_programs(0) - 1)
+    def _():
+        for t in range(tiles):
+            o_ref[:, t] = acc[t * bs:(t + 1) * bs].T.reshape(o_ref.shape[0], o_ref.shape[2], o_ref.shape[3])
 
 
-def tile_partials(tile_data, panels, slab_factor, n_aux):
+def tile_partials(tile_data, panels, slab_t, n_aux):
     tiles, n_p, bs, _ = tile_data.shape
     occ = panels.shape[2]
-    slab = slab_factor.shape[1]
+    slab = slab_t.shape[1]
     rows = slab // n_aux
     flops = tiles * (2 * n_p * bs * bs * occ + 2 * n_p * slab * occ * bs)
-    bytes_accessed = tile_data.size * 2 + panels.size * 2 + slab_factor.size * 2 + tiles * slab * bs * 4
+    bytes_accessed = tile_data.size * 2 + panels.size * 2 + slab_t.size * 2 + tiles * slab * bs * 4
     return pl.pallas_call(
         tile_kernel,
-        grid=(tiles,),
+        grid=(n_p // P_CHUNK,),
         in_specs=[
-            pl.BlockSpec((None, n_p, bs, bs), lambda t: (t, 0, 0, 0)),
-            pl.BlockSpec((None, bs, occ), lambda t: (t, 0, 0)),
-            pl.BlockSpec((n_p, slab, occ), lambda t: (0, 0, 0)),
+            pl.BlockSpec((tiles, P_CHUNK, bs, bs), lambda c: (0, c, 0, 0)),
+            pl.BlockSpec((tiles, bs, occ), lambda c: (0, 0, 0)),
+            pl.BlockSpec((P_CHUNK * occ, slab), lambda c: (c, 0)),
         ],
-        out_specs=pl.BlockSpec((n_aux, None, rows, bs), lambda t: (0, t, 0, 0)),
+        out_specs=pl.BlockSpec((n_aux, tiles, rows, bs), lambda c: (0, 0, 0, 0)),
         out_shape=jax.ShapeDtypeStruct((n_aux, tiles, rows, bs), jnp.float32),
+        scratch_shapes=[
+            pltpu.VMEM((tiles * bs, P_CHUNK * occ), jnp.bfloat16),
+            pltpu.VMEM((tiles * bs, slab), jnp.float32),
+        ],
+        compiler_params=pltpu.CompilerParams(vmem_limit_bytes=48 * 1024 * 1024),
         cost_estimate=pl.CostEstimate(flops=flops, transcendentals=0, bytes_accessed=bytes_accessed),
-    )(tile_data, panels, slab_factor)
+    )(tile_data, panels, slab_t)
 
 
 def local(three_center, slab_factor, coefficients, tile_owner, tile_block, tile_lam):
@@ -84,8 +97,10 @@
     send_panels = coef_blocks[lam_req.reshape(-1)].reshape(n_blk, per_group, bs, occ)
     panels = lax.all_to_all(send_panels, "blk", 0, 0, tiled=True).reshape(tiles, bs, occ)
 
-    partial = tile_partials(tile_data, panels, slab_factor, n_aux)
-    reduced = lax.psum_scatter(partial, "aux", scatter_dimension=0, tiled=True)[0]
+    n_p, slab = slab_factor.shape[0], slab_factor.shape[1]
+    slab_t = jnp.swapaxes(slab_factor, 1, 2).reshape(n_p * occ, slab)
+    partial = tile_partials(tile_data, panels, slab_t, n_aux)
+    reduced = jnp.sum(lax.all_to_all(partial, "aux", 0, 0, tiled=True), axis=0)
 
     picked = reduced[slot_tile]
     send_tiles = jnp.where(slot_valid[:, None, None], picked, 0.0)

time: 174 us -> 114 us (0.66)
  waiting for transfers between devices: 61.6 us -> 21.5 us
  Pallas kernels: 47.1 us -> 21.2 us
  between operations: 13.5 us -> 0.07 us
  blocking collectives: 35.9 us -> 45.8 us
  local copies, waits for them, and re-layouts: 4.32 us -> 10.8 us
  starting transfers between devices: 7.48 us -> 9.95 us
    reduce_scatter x1 -> x0, waiting for transfers between devices: 50.8 us -> none  [local(): lax.psum_scatter(partial, 'aux', scatter_dimension=0, tiled=True)[0]]
    pallas_call x1, Pallas kernels: 47.1 us -> 21.2 us  [tile_partials(): pl.pallas_call(tile_kernel, grid=(n_p // P_CHUNK,), in_specs=[pl.BlockSpe...]
    all_to_all x0 -> x1, waiting for transfers between devices: none -> 10.8 us  [local(): lax.all_to_all(send_panels, 'blk', 0, 0, tiled=True).reshape(tiles, bs, occ)]
    all_to_all x1, blocking collectives: 20.7 us -> 30.5 us  [local(): reduced = jnp.sum(lax.all_to_all(partial, 'aux', 0, 0, tiled=True), axis=0)]
    transpose x0 -> x1, local copies, waits for them, and re-layouts: none -> 6.42 us  [local(): slab_t = jnp.swapaxes(slab_factor, 1, 2).reshape(n_p * occ, slab)]
    all_to_all x0 -> x1, starting transfers between devices: none -> 4.11 us  [local(): lax.all_to_all(send_panels, 'blk', 0, 0, tiled=True).reshape(tiles, bs, occ)]
  transfers between devices with their start and end apart: 2 -> 2, of which waited for: 2 -> 2; matrix products, arithmetic and copies ran while one was open for 0% -> 6% of each run, Pallas kernels for 0% -> 0%
where the time goes in v2:
time: 114 us
  blocking collectives  45.8 us (40%)
  waiting for transfers between devices  21.5 us (19%)
  Pallas kernels  21.2 us (19%)
  local copies, waits for them, and re-layouts  10.8 us (9%)
  starting transfers between devices  9.95 us (9%)
  other arithmetic  4.43 us (4%)
    all_to_all x1, blocking collectives, local(): reduced = jnp.sum(lax.all_to_all(partial, 'aux', 0, 0, tiled=True), axis=0)  30.5 us
    pallas_call x1, Pallas kernels, tile_partials(): pl.pallas_call(tile_kernel, grid=(n_p // P_CHUNK,), in_specs=[pl.BlockSpe...  21.2 us
    all_to_all x1, blocking collectives, local(): ints_got = lax.all_to_all(ints, 'blk', 0, 0, tiled=True)  15.2 us
    all_to_all x1, waiting for transfers between devices, local(): received = lax.all_to_all(send_tiles, 'blk', 0, 0, tiled=True)  10.8 us
    all_to_all x1, waiting for transfers between devices, local(): lax.all_to_all(send_panels, 'blk', 0, 0, tiled=True).reshape(tiles, bs, occ)  10.8 us
    transpose x1, local copies, waits for them, and re-layouts, local(): slab_t = jnp.swapaxes(slab_factor, 1, 2).reshape(n_p * occ, slab)  6.42 us
    all_to_all x1, starting transfers between devices, local(): received = lax.all_to_all(send_tiles, 'blk', 0, 0, tiled=True)  5.85 us
    all_to_all x1, starting transfers between devices, local(): lax.all_to_all(send_panels, 'blk', 0, 0, tiled=True).reshape(tiles, bs, occ)  4.11 us
  transfers between devices with their start and end apart: 2, of which 2 were waited for; matrix products, arithmetic and copies ran while one was open for 6% of the time, Pallas kernels for 0%

profile of v2, /device:TPU:1, one launch (start us, length us, event | category | flops | bytes accessed | tf_op | source)
XLA Modules:
  0.0 113.7 jit_solution(2309347050423425821)
XLA Ops:
  0.0 0.0 copy-start
  0.0 0.9 convert_reduce_fusion
  0.9 0.7 multiply_add_fusion
  1.6 0.1 select_reduce_fusion.4
  1.7 0.1 fusion
  1.8 1.4 %gather_fusion = s32[32]{0:T(128)S(1)} fusion(s32[16]{0:T(128)} %bitcast.26, s32[1024]{0:T(1024)S(1)} %pad_clamp_fusion.1), kind=kCustom, calls=%fused_computation | custom fusion | bytes 384 | tf_op jit(solution)/shard_map/gather | solution.py:87
  3.1 0.1 gather.14
  3.2 0.1 reduce_or.12
  3.3 0.1 copy.29
  3.4 0.7 add_bitcast_fusion
  4.1 0.1 copy.30
  4.2 15.2 %all_to_all.27 = s32[16,1,3]{2,1,0:T(1,128)S(1)} all-to-all(s32[16,1,3]{2,1,0:T(1,128)S(1)} %copy.30), channel_id=1, replica_groups=mesh['blk'=16,'aux'=8] {'blk'}, dimensions={0} | all-to-all | bytes 384 | tf_op jit(solution)/shard_map/all_to_all | solution.py:92
  19.4 0.1 copy.31
  19.5 0.0 copy-done
  19.5 1.6 %gather_fusion.1 = bf16[16,128,256]{2,1,0:T(8,128)(2,1)} fusion(bf16[4,128,256]{2,1,0:T(8,128)(2,1)S(1)} %bitcast.24, s32[1024]{0:T(1024)S(1)} %pad_clamp_fusion), kind=kCustom, calls=%fused_computation.1 | custom fusion | bytes 2097216 | tf_op jit(solution)/shard_map/gather | solution.py:97
  21.1 4.1 %all-to-all-start.1 = ((bf16[16,1,128,256]{3,2,1,0:T(8,128)(2,1)}), bf16[16,1,128,256]{3,2,1,0:T(8,128)(2,1)S(1)}, u32[]{:S(2)}, u32[]{:S(2)}) async-start(bf16[16,1,128,256]{3,2,1,0:T(8,128)(2,1)} %bitcast.10), calls=%async_computation.1 | async-start | bytes 2097152 | tf_op jit(solution)/shard_map/all_to_all | solution.py:98
  25.2 6.4 %copy.33 = bf16[32,256,256]{2,1,0:T(8,128)(2,1)} copy(bf16[32,256,256]{1,2,0:T(8,128)(2,1)} %bitcast.27) | data formatting | bytes 8388608 | tf_op jit(solution)/shard_map/transpose | solution.py:101
  31.6 10.8 %all-to-all-done.1 = bf16[16,1,128,256]{3,2,1,0:T(8,128)(2,1)S(1)} async-done(((bf16[16,1,128,256]{3,2,1,0:T(8,128)(2,1)}), bf16[16,1,128,256]{3,2,1,0:T(8,128)(2,1)S(1)}, u32[]{:S(2)}, u32[]{:S(2)}) %all-to-all-start.1) | async-done | bytes 1048608 | tf_op jit(solution)/shard_map/all_to_all | solution.py:98
  42.4 21.2 %shard_map.64 = f32[8,16,32,128]{3,2,1,0:T(8,128)S(1)} custom-call(bf16[16,32,128,128]{3,2,1,0:T(8,128)(2,1)} %bitcast.37, bf16[16,128,256]{2,1,0:T(8,128)(2,1)S(1)} %bitcast.25, bf16[8192,256]{1,0:T(8,128)(2,1)} %bitcast.28), custom_call_target="tpu_custom_call" | custom-call | flops 12884901888 | bytes 24117248 | tf_op jit(solution)/shard_map/pallas_call | solution.py:47
  63.6 30.5 %all_to_all.28 = f32[8,16,32,128]{3,2,1,0:T(8,128)S(1)} all-to-all(f32[8,16,32,128]{3,2,1,0:T(8,128)S(1)} %shard_map.64), channel_id=1, replica_groups=mesh['blk'=16,'aux'=8] {'aux'}, dimensions={0} | all-to-all | bytes 4194304 | tf_op jit(solution)/shard_map/all_to_all | solution.py:103
  94.1 0.2 reduce_sum.68
  94.3 0.6 gather_fusion.2
  94.9 0.9 broadcast_select_fusion
  95.8 5.8 %all-to-all-start.3 = ((f32[16,2,32,128]{3,2,1,0:T(8,128)}), f32[16,2,32,128]{3,2,1,0:T(8,128)S(1)}, u32[]{:S(2)}, u32[]{:S(2)}) async-start(f32[16,2,32,128]{3,2,1,0:T(8,128)} %broadcast_select_fusion), calls=%async_computation.3 | async-start | bytes 1048576 | tf_op jit(solution)/shard_map/all_to_all | solution.py:108
  101.7 0.1 copy.32
  101.8 0.1 copy.34
  101.9 0.1 copy.35
  102.0 0.1 copy.36
  102.1 10.8 %all-to-all-done.3 = f32[16,2,32,128]{3,2,1,0:T(8,128)S(1)} async-done(((f32[16,2,32,128]{3,2,1,0:T(8,128)}), f32[16,2,32,128]{3,2,1,0:T(8,128)S(1)}, u32[]{:S(2)}, u32[]{:S(2)}) %all-to-all-start.3) | async-done | bytes 524320 | tf_op jit(solution)/shard_map/all_to_all | solution.py:108
  112.8 0.2 select_reduce_fusion.3
  113.1 0.6 pad_maximum_fusion
  (6 shorter events, 0.0 us)
Async XLA Ops:
  0.0 19.5 %copy-start = (bf16[512,256]{1,0:T(8,128)(2,1)S(1)}, bf16[512,256]{1,0:T(8,128)(2,1)}, u32[]{:S(2)}) copy-start(bf16[512,256]{1,0:T(8,128)(2,1)} %param.8) | copy-start | bytes 786436
  21.1 21.3 %all-to-all-start.1 = ((bf16[16,1,128,256]{3,2,1,0:T(8,128)(2,1)}), bf16[16,1,128,256]{3,2,1,0:T(8,128)(2,1)S(1)}, u32[]{:S(2)}, u32[]{:S(2)}) async-start(bf16[16,1,128,256]{3,2,1,0:T(8,128)(2,1)} %bitcast.10), calls=%async_computation.1 | async-start | bytes 2097152 | tf_op jit(solution)/shard_map/all_to_all | solution.py:98
  95.8 17.0 %all-to-all-start.3 = ((f32[16,2,32,128]{3,2,1,0:T(8,128)}), f32[16,2,32,128]{3,2,1,0:T(8,128)S(1)}, u32[]{:S(2)}, u32[]{:S(2)}) async-start(f32[16,2,32,128]{3,2,1,0:T(8,128)} %broadcast_select_fusion), calls=%async_computation.3 | async-start | bytes 1048576 | tf_op jit(solution)/shard_map/all_to_all | solution.py:108

commit v3 on v2

--- a/solution.py
+++ b/solution.py
@@ -8,7 +8,7 @@
 from jax.sharding import PartitionSpec as P
 
 CAP = 2
-P_CHUNK = 4
+P_CHUNK = 8
 ROW_CHUNK = 512
 
 
@@ -86,12 +86,7 @@
     slot_tile = jnp.sum(jnp.where(slot_hit, jnp.arange(tiles, dtype=jnp.int32)[None, :], 0), axis=1)
     slot_label = jnp.where(slot_valid, block_ids[slot_tile], -1)
 
-    ints = jnp.concatenate(
-        [lam_ids.reshape(n_blk, per_group), slot_label.reshape(n_blk, CAP)], axis=1
-    ).astype(jnp.int32)
-    ints_got = lax.all_to_all(ints, "blk", 0, 0, tiled=True)
-    lam_req = ints_got[:, :per_group]
-    got_labels = ints_got[:, per_group:]
+    lam_req = lax.all_to_all(lam_ids.reshape(n_blk, per_group), "blk", 0, 0, tiled=True)
 
     coef_blocks = coefficients.reshape(blocks_dev, bs, occ)
     send_panels = coef_blocks[lam_req.reshape(-1)].reshape(n_blk, per_group, bs, occ)
@@ -104,12 +99,16 @@
 
     picked = reduced[slot_tile]
     send_tiles = jnp.where(slot_valid[:, None, None], picked, 0.0)
+    label_rows = jnp.broadcast_to(slot_label.astype(jnp.float32)[:, None, None], (n_blk * CAP, 8, bs))
+    rows = send_tiles.shape[1]
+    send_tiles = jnp.concatenate([send_tiles, label_rows], axis=1)
     send_tiles = send_tiles.reshape((n_blk, CAP) + send_tiles.shape[1:])
     received = lax.all_to_all(send_tiles, "blk", 0, 0, tiled=True)
     received = received.reshape((n_blk * CAP,) + received.shape[2:])
-    labels = got_labels.reshape(-1)
+    labels = received[:, rows, 0]
+    data = received[:, :rows]
     owned = jnp.stack(
-        [jnp.sum(jnp.where((labels == b)[:, None, None], received, 0.0), axis=0) for b in range(blocks_dev)]
+        [jnp.sum(jnp.where((labels == b)[:, None, None], data, 0.0), axis=0) for b in range(blocks_dev)]
     )
     return owned
 

time: 114 us -> 116 us (1.018)
  waiting for transfers between devices: 21.5 us -> 35.2 us
  blocking collectives: 45.8 us -> 34 us
  Pallas kernels: 21.2 us -> 22.6 us
    all_to_all x1, waiting for transfers between devices: 10.8 us -> 24.5 us  [local(): reduced = jnp.sum(lax.all_to_all(partial, 'aux', 0, 0, tiled=True), axis=0)]
    all_to_all x2, blocking collectives: 45.8 us -> 34 us  [the longest x1 18.8 us: local(): received = lax.all_to_all(send_tiles, 'blk', 0, 0, tiled=True)]
    eq x1, other arithmetic: 0.01 us -> 2.37 us  [local(): labels == b]
    pallas_call x1, Pallas kernels: 21.2 us -> 22.6 us  [tile_partials(): pl.pallas_call(tile_kernel, grid=(n_p // P_CHUNK,), in_specs=[pl.BlockSpe...]
  transfers between devices with their start and end apart: 2 -> 2, of which waited for: 2 -> 2; matrix products, arithmetic and copies ran while one was open for 6% -> 7% of each run, Pallas kernels for 0% -> 0%
where the time goes in v3:
time: 116 us
  waiting for transfers between devices  35.2 us (30%)
  blocking collectives  34 us (29%)
  Pallas kernels  22.6 us (19%)
  local copies, waits for them, and re-layouts  10.3 us (9%)
  starting transfers between devices  9.34 us (8%)
  other arithmetic  4.38 us (4%)
    all_to_all x1, waiting for transfers between devices, local(): reduced = jnp.sum(lax.all_to_all(partial, 'aux', 0, 0, tiled=True), axis=0)  24.5 us
    pallas_call x1, Pallas kernels, tile_partials(): pl.pallas_call(tile_kernel, grid=(n_p // P_CHUNK,), in_specs=[pl.BlockSpe...  22.6 us
    all_to_all x1, blocking collectives, local(): received = lax.all_to_all(send_tiles, 'blk', 0, 0, tiled=True)  18.8 us
    all_to_all x1, blocking collectives, local(): lax.all_to_all(lam_ids.reshape(n_blk, per_group), 'blk', 0, 0, tiled=True)  15.2 us
    all_to_all x1, waiting for transfers between devices, local(): lax.all_to_all(send_panels, 'blk', 0, 0, tiled=True).reshape(tiles, bs, occ)  10.8 us
    transpose x1, local copies, waits for them, and re-layouts, local(): slab_t = jnp.swapaxes(slab_factor, 1, 2).reshape(n_p * occ, slab)  6.42 us
    all_to_all x1, starting transfers between devices, local(): reduced = jnp.sum(lax.all_to_all(partial, 'aux', 0, 0, tiled=True), axis=0)  5.23 us
    all_to_all x1, starting transfers between devices, local(): lax.all_to_all(send_panels, 'blk', 0, 0, tiled=True).reshape(tiles, bs, occ)  4.11 us
  transfers between devices with their start and end apart: 2, of which 2 were waited for; matrix products, arithmetic and copies ran while one was open for 7% of the time, Pallas kernels for 0%

profile of v3, /device:TPU:1, one launch (start us, length us, event | category | flops | bytes accessed | tf_op | source)
XLA Modules:
  0.0 116.0 jit_solution(8525925157362140827)
XLA Ops:
  0.0 0.0 copy-start
  0.0 0.8 copy.14
  0.8 15.2 %all_to_all.27 = s32[16,1,1]{2,1,0:T(1,128)S(1)} all-to-all(s32[16,1,1]{2,1,0:T(1,128)S(1)} %copy.14), channel_id=1, replica_groups=mesh['blk'=16,'aux'=8] {'blk'}, dimensions={0} | all-to-all | bytes 128 | tf_op jit(solution)/shard_map/all_to_all | solution.py:89
  16.0 0.4 reduce
  16.4 0.0 copy-done
  16.4 1.6 %gather_fusion = bf16[16,128,256]{2,1,0:T(8,128)(2,1)} fusion(bf16[4,128,256]{2,1,0:T(8,128)(2,1)S(1)} %bitcast.24, s32[1024]{0:T(1024)S(1)} %pad_clamp_fusion.1), kind=kCustom, calls=%fused_computation | custom fusion | bytes 2097216 | tf_op jit(solution)/shard_map/gather | solution.py:92
  18.0 4.1 %all-to-all-start.1 = ((bf16[16,1,128,256]{3,2,1,0:T(8,128)(2,1)}), bf16[16,1,128,256]{3,2,1,0:T(8,128)(2,1)S(1)}, u32[]{:S(2)}, u32[]{:S(2)}) async-start(bf16[16,1,128,256]{3,2,1,0:T(8,128)(2,1)} %bitcast.5), calls=%async_computation.1 | async-start | bytes 2097152 | tf_op jit(solution)/shard_map/all_to_all | solution.py:93
  22.1 6.4 %copy.15 = bf16[32,256,256]{2,1,0:T(8,128)(2,1)} copy(bf16[32,256,256]{1,2,0:T(8,128)(2,1)} %bitcast.27) | data formatting | bytes 8388608 | tf_op jit(solution)/shard_map/transpose | solution.py:96
  28.5 10.8 %all-to-all-done.1 = bf16[16,1,128,256]{3,2,1,0:T(8,128)(2,1)S(1)} async-done(((bf16[16,1,128,256]{3,2,1,0:T(8,128)(2,1)}), bf16[16,1,128,256]{3,2,1,0:T(8,128)(2,1)S(1)}, u32[]{:S(2)}, u32[]{:S(2)}) %all-to-all-start.1) | async-done | bytes 1048608 | tf_op jit(solution)/shard_map/all_to_all | solution.py:93
  39.3 22.6 %shard_map.64 = f32[8,16,32,128]{3,2,1,0:T(8,128)} custom-call(bf16[16,32,128,128]{3,2,1,0:T(8,128)(2,1)} %bitcast.37, bf16[16,128,256]{2,1,0:T(8,128)(2,1)S(1)} %bitcast.25, bf16[8192,256]{1,0:T(8,128)(2,1)} %bitcast.28), custom_call_target="tpu_custom_call" | custom-call | flops 12884901888 | bytes 24117248 | tf_op jit(solution)/shard_map/pallas_call | solution.py:47
  61.9 0.0 copy-start.2
  61.9 0.0 copy-start.1
  61.9 5.2 %all-to-all-start.2 = ((f32[8,16,32,128]{3,2,1,0:T(8,128)}), f32[8,16,32,128]{3,2,1,0:T(8,128)S(1)}, u32[]{:S(2)}, u32[]{:S(2)}) async-start(f32[8,16,32,128]{3,2,1,0:T(8,128)} %shard_map.64), calls=%async_computation.2 | async-start | bytes 4194304 | tf_op jit(solution)/shard_map/all_to_all | solution.py:98
  67.1 0.0 copy-done.2
  67.1 0.2 convert_reduce_fusion
  67.3 0.1 fusion
  67.4 0.1 broadcast_in_dim.83
  67.5 0.1 select_reduce_fusion.4
  67.6 0.0 copy-done.1
  67.6 0.7 gather_fusion.2
  68.3 0.1 gather.17
  68.4 24.5 %all-to-all-done.2 = f32[8,16,32,128]{3,2,1,0:T(8,128)S(1)} async-done(((f32[8,16,32,128]{3,2,1,0:T(8,128)}), f32[8,16,32,128]{3,2,1,0:T(8,128)S(1)}, u32[]{:S(2)}, u32[]{:S(2)}) %all-to-all-start.2) | async-done | bytes 2097184 | tf_op jit(solution)/shard_map/all_to_all | solution.py:98
  92.9 0.2 reduce_sum.66
  93.1 0.6 gather_fusion.1
  93.7 0.1 broadcast_select_fusion
  93.8 0.1 broadcast_in_dim.89
  93.9 0.1 pad_maximum_fusion
  94.0 18.8 %all_to_all.28 = f32[16,2,40,128]{3,2,1,0:T(8,128)S(1)} all-to-all(f32[16,2,40,128]{3,2,1,0:T(8,128)S(1)} %pad_maximum_fusion), channel_id=1, replica_groups=mesh['blk'=16,'aux'=8] {'blk'}, dimensions={0} | all-to-all | bytes 1310720 | tf_op jit(solution)/shard_map/all_to_all | solution.py:106
  112.8 2.4 %compare_reduce_fusion.3 = (pred[32]{0:T(512)(128)(4,1)S(1)}, pred[32]{0:T(512)(128)(4,1)S(1)}, pred[32]{0:T(512)(128)(4,1)S(1)}, pred[32]{0:T(512)(128)(4,1)S(1)}) fusion(f32[32,40,128]{2,1,0:T(8,128)S(1)} %bitcast.29), kind=kLoop, calls=%fused_computation.13 | loop fusion | flops 128 | bytes 256 | tf_op jit(solution)/shard_map/eq | solution.py:111
  115.1 0.2 select_reduce_fusion.3
  115.4 0.6 pad_maximum_fusion.1
  (6 shorter events, 0.0 us)
Async XLA Ops:
  0.0 16.4 %copy-start = (bf16[512,256]{1,0:T(8,128)(2,1)S(1)}, bf16[512,256]{1,0:T(8,128)(2,1)}, u32[]{:S(2)}) copy-start(bf16[512,256]{1,0:T(8,128)(2,1)} %param.8) | copy-start | bytes 786436
  18.0 21.3 %all-to-all-start.1 = ((bf16[16,1,128,256]{3,2,1,0:T(8,128)(2,1)}), bf16[16,1,128,256]{3,2,1,0:T(8,128)(2,1)S(1)}, u32[]{:S(2)}, u32[]{:S(2)}) async-start(bf16[16,1,128,256]{3,2,1,0:T(8,128)(2,1)} %bitcast.5), calls=%async_computation.1 | async-start | bytes 2097152 | tf_op jit(solution)/shard_map/all_to_all | solution.py:93
  61.9 5.2 %copy-start.2 = (s32[1,16,1]{1,2,0:T(1,128)S(1)}, s32[1,16,1]{1,2,0:T(1,128)}, u32[]{:S(2)}) copy-start(s32[1,16,1]{1,2,0:T(1,128)} %param.9) | copy-start | bytes 196
  61.9 5.7 %copy-start.1 = (s32[1,16]{1,0:T(1,128)S(1)}, s32[1,16]{1,0:T(1,128)}, u32[]{:S(2)}) copy-start(s32[1,16]{1,0:T(1,128)} %param.10) | copy-start | bytes 196
  61.9 31.0 %all-to-all-start.2 = ((f32[8,16,32,128]{3,2,1,0:T(8,128)}), f32[8,16,32,128]{3,2,1,0:T(8,128)S(1)}, u32[]{:S(2)}, u32[]{:S(2)}) async-start(f32[8,16,32,128]{3,2,1,0:T(8,128)} %shard_map.64), calls=%async_computation.2 | async-start | bytes 4194304 | tf_op jit(solution)/shard_map/all_to_all | solution.py:98

commit v4 on v2

--- a/solution.py
+++ b/solution.py
@@ -84,14 +84,8 @@
     slot_hit = jnp.arange(n_blk * CAP, dtype=jnp.int32)[:, None] == position[None, :]
     slot_valid = jnp.any(slot_hit, axis=1)
     slot_tile = jnp.sum(jnp.where(slot_hit, jnp.arange(tiles, dtype=jnp.int32)[None, :], 0), axis=1)
-    slot_label = jnp.where(slot_valid, block_ids[slot_tile], -1)
 
-    ints = jnp.concatenate(
-        [lam_ids.reshape(n_blk, per_group), slot_label.reshape(n_blk, CAP)], axis=1
-    ).astype(jnp.int32)
-    ints_got = lax.all_to_all(ints, "blk", 0, 0, tiled=True)
-    lam_req = ints_got[:, :per_group]
-    got_labels = ints_got[:, per_group:]
+    lam_req = lax.all_to_all(lam_ids.reshape(n_blk, per_group), "blk", 0, 0, tiled=True)
 
     coef_blocks = coefficients.reshape(blocks_dev, bs, occ)
     send_panels = coef_blocks[lam_req.reshape(-1)].reshape(n_blk, per_group, bs, occ)
@@ -102,12 +96,19 @@
     partial = tile_partials(tile_data, panels, slab_t, n_aux)
     reduced = jnp.sum(lax.all_to_all(partial, "aux", 0, 0, tiled=True), axis=0)
 
+    me = lax.axis_index("blk")
+    lists = lax.all_gather(jnp.stack([owner_ids, block_ids]), "blk", axis=0, tiled=False)
+    all_owner, all_block = lists[:, 0], lists[:, 1]
+    all_earlier = jnp.arange(tiles)[None, None, :] < jnp.arange(tiles)[None, :, None]
+    all_rank = jnp.sum(((all_owner[:, :, None] == all_owner[:, None, :]) & all_earlier).astype(jnp.int32), axis=2)
+    mine = (all_owner == me)[:, None, :] & (all_rank[:, None, :] == jnp.arange(CAP)[None, :, None])
+    labels = (jnp.sum(jnp.where(mine, all_block[:, None, :] + 1, 0), axis=2) - 1).reshape(-1)
+
     picked = reduced[slot_tile]
     send_tiles = jnp.where(slot_valid[:, None, None], picked, 0.0)
     send_tiles = send_tiles.reshape((n_blk, CAP) + send_tiles.shape[1:])
     received = lax.all_to_all(send_tiles, "blk", 0, 0, tiled=True)
     received = received.reshape((n_blk * CAP,) + received.shape[2:])
-    labels = got_labels.reshape(-1)
     owned = jnp.stack(
         [jnp.sum(jnp.where((labels == b)[:, None, None], received, 0.0), axis=0) for b in range(blocks_dev)]
     )

time: 114 us -> 127 us (1.11)
  blocking collectives: 45.8 us -> 55.7 us
  starting transfers between devices: 9.95 us -> 12.9 us
  Pallas kernels: 21.2 us -> 22.5 us
    all_gather x0 -> x1, blocking collectives: none -> 40.5 us  [local(): lax.all_gather(jnp.stack([owner_ids, block_ids]), 'blk', axis=0, tiled=Fa...]
    all_to_all x2 -> x1, blocking collectives: 45.8 us -> 15.2 us  [local(): lax.all_to_all(lam_ids.reshape(n_blk, per_group), 'blk', 0, 0, tiled=True)]
    all_to_all x0 -> x1, starting transfers between devices: none -> 5.23 us  [local(): reduced = jnp.sum(lax.all_to_all(partial, 'aux', 0, 0, tiled=True), axis=0)]
    all_to_all x1, starting transfers between devices: 5.85 us -> 3.53 us  [local(): received = lax.all_to_all(send_tiles, 'blk', 0, 0, tiled=True)]
    gather x2 -> x0, local copies, waits for them, and re-layouts: 1.44 us -> none  [local(): slot_label = jnp.where(slot_valid, block_ids[slot_tile], -1)]
    pallas_call x1, Pallas kernels: 21.2 us -> 22.5 us  [tile_partials(): pl.pallas_call(tile_kernel, grid=(n_p // P_CHUNK,), in_specs=[pl.BlockSpe...]
  transfers between devices with their start and end apart: 2 -> 3, of which waited for: 2 -> 2; matrix products, arithmetic and copies ran while one was open for 6% -> 6% of each run, Pallas kernels for 0% -> 0%
where the time goes in v4:
time: 127 us; the launch traced here: 125 us
  blocking collectives  55.7 us (44%)
  Pallas kernels  22.5 us (18%)
  waiting for transfers between devices  21 us (17%)
  starting transfers between devices  12.9 us (10%)
  local copies, waits for them, and re-layouts  9.87 us (8%)
  other arithmetic  3.33 us (3%)
    all_gather x1, blocking collectives, local(): lax.all_gather(jnp.stack([owner_ids, block_ids]), 'blk', axis=0, tiled=Fa...  40.5 us
    pallas_call x1, Pallas kernels, tile_partials(): pl.pallas_call(tile_kernel, grid=(n_p // P_CHUNK,), in_specs=[pl.BlockSpe...  22.5 us
    all_to_all x1, blocking collectives, local(): lax.all_to_all(lam_ids.reshape(n_blk, per_group), 'blk', 0, 0, tiled=True)  15.2 us
    all_to_all x1, waiting for transfers between devices, local(): lax.all_to_all(send_panels, 'blk', 0, 0, tiled=True).reshape(tiles, bs, occ)  10.8 us
    all_to_all x1, waiting for transfers between devices, local(): received = lax.all_to_all(send_tiles, 'blk', 0, 0, tiled=True)  10.3 us
    transpose x1, local copies, waits for them, and re-layouts, local(): slab_t = jnp.swapaxes(slab_factor, 1, 2).reshape(n_p * occ, slab)  6.42 us
    all_to_all x1, starting transfers between devices, local(): reduced = jnp.sum(lax.all_to_all(partial, 'aux', 0, 0, tiled=True), axis=0)  5.23 us
    all_to_all x1, starting transfers between devices, local(): lax.all_to_all(send_panels, 'blk', 0, 0, tiled=True).reshape(tiles, bs, occ)  4.11 us
  transfers between devices with their start and end apart: 3, of which 2 were waited for; matrix products, arithmetic and copies ran while one was open for 6% of the time, Pallas kernels for 0%

profile of v4, /device:TPU:1, one launch (start us, length us, event | category | flops | bytes accessed | tf_op | source)
XLA Modules:
  0.0 125.5 jit_solution(14176316385137489286)
XLA Ops:
  0.0 0.0 copy-start
  0.0 0.8 copy.17
  0.8 15.2 %all_to_all.27 = s32[16,1,1]{2,1,0:T(1,128)S(1)} all-to-all(s32[16,1,1]{2,1,0:T(1,128)S(1)} %copy.17), channel_id=1, replica_groups=mesh['blk'=16,'aux'=8] {'blk'}, dimensions={0} | all-to-all | bytes 128 | tf_op jit(solution)/shard_map/all_to_all | solution.py:88
  16.0 0.4 reduce.4
  16.4 0.0 copy-done
  16.4 1.6 %gather_fusion = bf16[16,128,256]{2,1,0:T(8,128)(2,1)} fusion(bf16[4,128,256]{2,1,0:T(8,128)(2,1)S(1)} %bitcast.31, s32[1024]{0:T(1024)S(1)} %pad_clamp_fusion.1), kind=kCustom, calls=%fused_computation | custom fusion | bytes 2097216 | tf_op jit(solution)/shard_map/gather | solution.py:91
  18.0 4.1 %all-to-all-start.1 = ((bf16[16,1,128,256]{3,2,1,0:T(8,128)(2,1)}), bf16[16,1,128,256]{3,2,1,0:T(8,128)(2,1)S(1)}, u32[]{:S(2)}, u32[]{:S(2)}) async-start(bf16[16,1,128,256]{3,2,1,0:T(8,128)(2,1)} %bitcast.10), calls=%async_computation.1 | async-start | bytes 2097152 | tf_op jit(solution)/shard_map/all_to_all | solution.py:92
  22.1 6.4 %copy.18 = bf16[32,256,256]{2,1,0:T(8,128)(2,1)} copy(bf16[32,256,256]{1,2,0:T(8,128)(2,1)} %bitcast.33) | data formatting | bytes 8388608 | tf_op jit(solution)/shard_map/transpose | solution.py:95
  28.5 10.8 %all-to-all-done.1 = bf16[16,1,128,256]{3,2,1,0:T(8,128)(2,1)S(1)} async-done(((bf16[16,1,128,256]{3,2,1,0:T(8,128)(2,1)}), bf16[16,1,128,256]{3,2,1,0:T(8,128)(2,1)S(1)}, u32[]{:S(2)}, u32[]{:S(2)}) %all-to-all-start.1) | async-done | bytes 1048608 | tf_op jit(solution)/shard_map/all_to_all | solution.py:92
  39.3 22.5 %shard_map.64 = f32[8,16,32,128]{3,2,1,0:T(8,128)} custom-call(bf16[16,32,128,128]{3,2,1,0:T(8,128)(2,1)} %bitcast.46, bf16[16,128,256]{2,1,0:T(8,128)(2,1)S(1)} %bitcast.32, bf16[8192,256]{1,0:T(8,128)(2,1)} %bitcast.34), custom_call_target="tpu_custom_call" | custom-call | flops 12884901888 | bytes 24117248 | tf_op jit(solution)/shard_map/pallas_call | solution.py:47
  61.8 0.0 copy-start.1
  61.8 0.0 copy-start.2
  61.8 5.2 %all-to-all-start.2 = ((f32[8,16,32,128]{3,2,1,0:T(8,128)}), f32[8,16,32,128]{3,2,1,0:T(8,128)S(1)}, u32[]{:S(2)}, u32[]{:S(2)}) async-start(f32[8,16,32,128]{3,2,1,0:T(8,128)} %shard_map.64), calls=%async_computation.2 | async-start | bytes 4194304 | tf_op jit(solution)/shard_map/all_to_all | solution.py:97
  67.0 0.0 copy-done.1
  67.0 0.2 convert_reduce_fusion.1
  67.2 0.1 fusion.1
  67.3 0.1 broadcast_in_dim.85
  67.4 0.0 copy-done.2
  67.5 40.5 %all-gather.1 = s32[16,2,16]{2,1,0:T(2,128)S(1)} all-gather(s32[1,2,16]{2,1,0:T(2,128)S(1)} %add_bitcast_fusion), channel_id=2, replica_groups=mesh['blk'=16,'aux'=8] {'blk'}, dimensions={0}, use_global_device_ids=true | all-gather | bytes 2176 | tf_op jit(solution)/shard_map/all_gather | solution.py:100
  108.0 0.1 select_reduce_fusion.5
  108.1 0.0 all-to-all-done.2
  108.1 0.2 reduce_sum.86
  108.3 0.6 gather_fusion.1
  108.9 0.9 broadcast_select_fusion
  109.8 3.5 %all-to-all-start.3 = ((f32[16,2,32,128]{3,2,1,0:T(8,128)}), f32[16,2,32,128]{3,2,1,0:T(8,128)S(1)}, u32[]{:S(2)}, u32[]{:S(2)}) async-start(f32[16,2,32,128]{3,2,1,0:T(8,128)} %broadcast_select_fusion), calls=%async_computation.3 | async-start | bytes 1048576 | tf_op jit(solution)/shard_map/all_to_all | solution.py:110
  113.4 0.4 convert_reduce_fusion
  113.8 0.1 select_reduce_fusion.4
  113.9 0.1 copy.16
  114.0 0.1 copy.21
  114.1 0.1 copy.20
  114.2 0.1 copy.19
  114.3 10.3 %all-to-all-done.3 = f32[16,2,32,128]{3,2,1,0:T(8,128)S(1)} async-done(((f32[16,2,32,128]{3,2,1,0:T(8,128)}), f32[16,2,32,128]{3,2,1,0:T(8,128)S(1)}, u32[]{:S(2)}, u32[]{:S(2)}) %all-to-all-start.3) | async-done | bytes 524320 | tf_op jit(solution)/shard_map/all_to_all | solution.py:110
  124.6 0.2 select_reduce_fusion.3
  124.9 0.6 pad_maximum_fusion
  (10 shorter events, 0.1 us)
Async XLA Ops:
  0.0 16.4 %copy-start = (bf16[512,256]{1,0:T(8,128)(2,1)S(1)}, bf16[512,256]{1,0:T(8,128)(2,1)}, u32[]{:S(2)}) copy-start(bf16[512,256]{1,0:T(8,128)(2,1)} %param.8) | copy-start | bytes 786436
  18.0 21.3 %all-to-all-start.1 = ((bf16[16,1,128,256]{3,2,1,0:T(8,128)(2,1)}), bf16[16,1,128,256]{3,2,1,0:T(8,128)(2,1)S(1)}, u32[]{:S(2)}, u32[]{:S(2)}) async-start(bf16[16,1,128,256]{3,2,1,0:T(8,128)(2,1)} %bitcast.10), calls=%async_computation.1 | async-start | bytes 2097152 | tf_op jit(solution)/shard_map/all_to_all | solution.py:92
  61.8 5.2 %copy-start.1 = (s32[1,16,1]{1,2,0:T(1,128)S(1)}, s32[1,16,1]{1,2,0:T(1,128)}, u32[]{:S(2)}) copy-start(s32[1,16,1]{1,2,0:T(1,128)} %param.9) | copy-start | bytes 196
  61.8 5.6 %copy-start.2 = (s32[1,16]{1,0:T(1,128)S(1)}, s32[1,16]{1,0:T(1,128)}, u32[]{:S(2)}) copy-start(s32[1,16]{1,0:T(1,128)} %param.10) | copy-start | bytes 196
  61.8 46.3 %all-to-all-start.2 = ((f32[8,16,32,128]{3,2,1,0:T(8,128)}), f32[8,16,32,128]{3,2,1,0:T(8,128)S(1)}, u32[]{:S(2)}, u32[]{:S(2)}) async-start(f32[8,16,32,128]{3,2,1,0:T(8,128)} %shard_map.64), calls=%async_computation.2 | async-start | bytes 4194304 | tf_op jit(solution)/shard_map/all_to_all | solution.py:97
  109.8 14.8 %all-to-all-start.3 = ((f32[16,2,32,128]{3,2,1,0:T(8,128)}), f32[16,2,32,128]{3,2,1,0:T(8,128)S(1)}, u32[]{:S(2)}, u32[]{:S(2)}) async-start(f32[16,2,32,128]{3,2,1,0:T(8,128)} %broadcast_select_fusion), calls=%async_computation.3 | async-start | bytes 1048576 | tf_op jit(solution)/shard_map/all_to_all | solution.py:110

commit v5 on v4

--- a/solution.py
+++ b/solution.py
@@ -77,15 +77,12 @@
     block_ids = tile_block[0]
     lam_ids = tile_lam[0]
 
-    same_owner = owner_ids[:, None] == owner_ids[None, :]
-    earlier = jnp.arange(tiles)[None, :] < jnp.arange(tiles)[:, None]
-    slot_rank = jnp.sum((same_owner & earlier).astype(jnp.int32), axis=1)
-    position = owner_ids * CAP + slot_rank
-    slot_hit = jnp.arange(n_blk * CAP, dtype=jnp.int32)[:, None] == position[None, :]
-    slot_valid = jnp.any(slot_hit, axis=1)
-    slot_tile = jnp.sum(jnp.where(slot_hit, jnp.arange(tiles, dtype=jnp.int32)[None, :], 0), axis=1)
-
-    lam_req = lax.all_to_all(lam_ids.reshape(n_blk, per_group), "blk", 0, 0, tiled=True)
+    lists = jnp.broadcast_to(jnp.concatenate([owner_ids, block_ids])[None, :], (n_blk, 2 * tiles))
+    ints = jnp.concatenate([lam_ids.reshape(n_blk, per_group), lists], axis=1).astype(jnp.int32)
+    ints_got = lax.all_to_all(ints, "blk", 0, 0, tiled=True)
+    lam_req = ints_got[:, :per_group]
+    all_owner = ints_got[:, per_group:per_group + tiles]
+    all_block = ints_got[:, per_group + tiles:]
 
     coef_blocks = coefficients.reshape(blocks_dev, bs, occ)
     send_panels = coef_blocks[lam_req.reshape(-1)].reshape(n_blk, per_group, bs, occ)
@@ -96,11 +93,16 @@
     partial = tile_partials(tile_data, panels, slab_t, n_aux)
     reduced = jnp.sum(lax.all_to_all(partial, "aux", 0, 0, tiled=True), axis=0)
 
+    same_owner = owner_ids[:, None] == owner_ids[None, :]
+    earlier = jnp.arange(tiles)[None, :] < jnp.arange(tiles)[:, None]
+    slot_rank = jnp.sum((same_owner & earlier).astype(jnp.int32), axis=1)
+    position = owner_ids * CAP + slot_rank
+    slot_hit = jnp.arange(n_blk * CAP, dtype=jnp.int32)[:, None] == position[None, :]
+    slot_valid = jnp.any(slot_hit, axis=1)
+    slot_tile = jnp.sum(jnp.where(slot_hit, jnp.arange(tiles, dtype=jnp.int32)[None, :], 0), axis=1)
+
     me = lax.axis_index("blk")
-    lists = lax.all_gather(jnp.stack([owner_ids, block_ids]), "blk", axis=0, tiled=False)
-    all_owner, all_block = lists[:, 0], lists[:, 1]
-    all_earlier = jnp.arange(tiles)[None, None, :] < jnp.arange(tiles)[None, :, None]
-    all_rank = jnp.sum(((all_owner[:, :, None] == all_owner[:, None, :]) & all_earlier).astype(jnp.int32), axis=2)
+    all_rank = jnp.sum(((all_owner[:, :, None] == all_owner[:, None, :]) & earlier[None]).astype(jnp.int32), axis=2)
     mine = (all_owner == me)[:, None, :] & (all_rank[:, None, :] == jnp.arange(CAP)[None, :, None])
     labels = (jnp.sum(jnp.where(mine, all_block[:, None, :] + 1, 0), axis=2) - 1).reshape(-1)
 

time: 127 us -> 113 us (0.89); the launches traced: 125 us -> 113 us
  blocking collectives: 55.7 us -> 15.2 us
  waiting for transfers between devices: 21 us -> 46.1 us
  starting transfers between devices: 12.9 us -> 15.1 us
    all_gather x1 -> x0, blocking collectives: 40.5 us -> none  [local(): lax.all_gather(jnp.stack([owner_ids, block_ids]), 'blk', axis=0, tiled=Fa...]
    all_to_all x1, waiting for transfers between devices: 0.01 us -> 25.2 us  [local(): reduced = jnp.sum(lax.all_to_all(partial, 'aux', 0, 0, tiled=True), axis=0)]
    all_to_all x1, starting transfers between devices: 3.53 us -> 5.77 us  [local(): received = lax.all_to_all(send_tiles, 'blk', 0, 0, tiled=True)]
  transfers between devices with their start and end apart: 3 -> 3, of which waited for: 2 -> 3; matrix products, arithmetic and copies ran while one was open for 6% -> 7% of each run, Pallas kernels for 0% -> 0%
where the time goes in v5:
time: 113 us
  waiting for transfers between devices  46.1 us (41%)
  Pallas kernels  22.5 us (20%)
  blocking collectives  15.2 us (13%)
  starting transfers between devices  15.1 us (13%)
  local copies, waits for them, and re-layouts  9.94 us (9%)
  other arithmetic  3.93 us (3%)
    all_to_all x1, waiting for transfers between devices, local(): reduced = jnp.sum(lax.all_to_all(partial, 'aux', 0, 0, tiled=True), axis=0)  25.2 us
    pallas_call x1, Pallas kernels, tile_partials(): pl.pallas_call(tile_kernel, grid=(n_p // P_CHUNK,), in_specs=[pl.BlockSpe...  22.5 us
    all_to_all x1, blocking collectives, local(): ints_got = lax.all_to_all(ints, 'blk', 0, 0, tiled=True)  15.2 us
    all_to_all x1, waiting for transfers between devices, local(): lax.all_to_all(send_panels, 'blk', 0, 0, tiled=True).reshape(tiles, bs, occ)  10.8 us
    all_to_all x1, waiting for transfers between devices, local(): received = lax.all_to_all(send_tiles, 'blk', 0, 0, tiled=True)  10.1 us
    transpose x1, local copies, waits for them, and re-layouts, local(): slab_t = jnp.swapaxes(slab_factor, 1, 2).reshape(n_p * occ, slab)  6.42 us
    all_to_all x1, starting transfers between devices, local(): received = lax.all_to_all(send_tiles, 'blk', 0, 0, tiled=True)  5.77 us
    all_to_all x1, starting transfers between devices, local(): reduced = jnp.sum(lax.all_to_all(partial, 'aux', 0, 0, tiled=True), axis=0)  5.23 us
  transfers between devices with their start and end apart: 3, of which 3 were waited for; matrix products, arithmetic and copies ran while one was open for 7% of the time, Pallas kernels for 0%

profile of v5, /device:TPU:1, one launch (start us, length us, event | category | flops | bytes accessed | tf_op | source)
XLA Modules:
  0.0 112.9 jit_solution(4177531352217310053)
XLA Ops:
  0.0 0.0 copy-start
  0.0 0.8 copy.21
  0.8 0.7 pad_add_fusion.1
  1.5 0.1 pad.5.clone
  1.6 15.2 %all_to_all.27 = s32[16,1,33]{2,1,0:T(1,128)S(1)} all-to-all(s32[16,1,33]{2,1,0:T(1,128)S(1)} %bitcast.33), channel_id=1, replica_groups=mesh['blk'=16,'aux'=8] {'blk'}, dimensions={0} | all-to-all | bytes 4224 | tf_op jit(solution)/shard_map/all_to_all | solution.py:82
  16.8 0.1 fusion.1
  17.0 0.0 copy-done
  17.0 1.6 %gather_fusion = bf16[16,128,256]{2,1,0:T(8,128)(2,1)} fusion(bf16[4,128,256]{2,1,0:T(8,128)(2,1)S(1)} %bitcast.21, s32[1024]{0:T(1024)S(1)} %pad_clamp_fusion.1), kind=kCustom, calls=%fused_computation | custom fusion | bytes 2097216 | tf_op jit(solution)/shard_map/gather | solution.py:88
  18.6 4.1 %all-to-all-start.1 = ((bf16[16,1,128,256]{3,2,1,0:T(8,128)(2,1)}), bf16[16,1,128,256]{3,2,1,0:T(8,128)(2,1)S(1)}, u32[]{:S(2)}, u32[]{:S(2)}) async-start(bf16[16,1,128,256]{3,2,1,0:T(8,128)(2,1)} %bitcast.7), calls=%async_computation.1 | async-start | bytes 2097152 | tf_op jit(solution)/shard_map/all_to_all | solution.py:89
  22.7 6.4 %copy.23 = bf16[32,256,256]{2,1,0:T(8,128)(2,1)} copy(bf16[32,256,256]{1,2,0:T(8,128)(2,1)} %bitcast.23) | data formatting | bytes 8388608 | tf_op jit(solution)/shard_map/transpose | solution.py:92
  29.1 10.8 %all-to-all-done.1 = bf16[16,1,128,256]{3,2,1,0:T(8,128)(2,1)S(1)} async-done(((bf16[16,1,128,256]{3,2,1,0:T(8,128)(2,1)}), bf16[16,1,128,256]{3,2,1,0:T(8,128)(2,1)S(1)}, u32[]{:S(2)}, u32[]{:S(2)}) %all-to-all-start.1) | async-done | bytes 1048608 | tf_op jit(solution)/shard_map/all_to_all | solution.py:89
  39.8 22.5 %shard_map.64 = f32[8,16,32,128]{3,2,1,0:T(8,128)} custom-call(bf16[16,32,128,128]{3,2,1,0:T(8,128)(2,1)} %bitcast.35, bf16[16,128,256]{2,1,0:T(8,128)(2,1)S(1)} %bitcast.22, bf16[8192,256]{1,0:T(8,128)(2,1)} %bitcast.24), custom_call_target="tpu_custom_call" | custom-call | flops 12884901888 | bytes 24117248 | tf_op jit(solution)/shard_map/pallas_call | solution.py:47
  62.4 0.0 copy-start.1
  62.4 5.2 %all-to-all-start.2 = ((f32[8,16,32,128]{3,2,1,0:T(8,128)}), f32[8,16,32,128]{3,2,1,0:T(8,128)S(1)}, u32[]{:S(2)}, u32[]{:S(2)}) async-start(f32[8,16,32,128]{3,2,1,0:T(8,128)} %shard_map.64), calls=%async_computation.2 | async-start | bytes 4194304 | tf_op jit(solution)/shard_map/all_to_all | solution.py:94
  67.6 0.0 copy-done.1
  67.6 0.2 convert_reduce_fusion.1
  67.8 0.1 fusion.2
  67.9 0.1 broadcast_in_dim.91
  68.0 0.1 select_reduce_fusion.5
  68.1 0.1 fusion.4
  68.2 25.2 %all-to-all-done.2 = f32[8,16,32,128]{3,2,1,0:T(8,128)S(1)} async-done(((f32[8,16,32,128]{3,2,1,0:T(8,128)}), f32[8,16,32,128]{3,2,1,0:T(8,128)S(1)}, u32[]{:S(2)}, u32[]{:S(2)}) %all-to-all-start.2) | async-done | bytes 2097184 | tf_op jit(solution)/shard_map/all_to_all | solution.py:94
  93.4 0.2 reduce_sum.86
  93.6 0.6 gather_fusion.1
  94.2 0.9 broadcast_select_fusion
  95.1 5.8 %all-to-all-start.3 = ((f32[16,2,32,128]{3,2,1,0:T(8,128)}), f32[16,2,32,128]{3,2,1,0:T(8,128)S(1)}, u32[]{:S(2)}, u32[]{:S(2)}) async-start(f32[16,2,32,128]{3,2,1,0:T(8,128)} %broadcast_select_fusion), calls=%async_computation.3 | async-start | bytes 1048576 | tf_op jit(solution)/shard_map/all_to_all | solution.py:112
  100.8 0.1 broadcast_compare_fusion
  100.9 0.4 convert_reduce_fusion
  101.3 0.1 select_reduce_fusion.4
  101.5 0.1 copy.22
  101.6 0.1 copy.24
  101.7 0.1 copy.25
  101.8 0.1 copy.26
  101.9 10.1 %all-to-all-done.3 = f32[16,2,32,128]{3,2,1,0:T(8,128)S(1)} async-done(((f32[16,2,32,128]{3,2,1,0:T(8,128)}), f32[16,2,32,128]{3,2,1,0:T(8,128)S(1)}, u32[]{:S(2)}, u32[]{:S(2)}) %all-to-all-start.3) | async-done | bytes 524320 | tf_op jit(solution)/shard_map/all_to_all | solution.py:112
  112.0 0.2 select_reduce_fusion.3
  112.2 0.6 pad_maximum_fusion
  (7 shorter events, 0.1 us)
Async XLA Ops:
  0.0 17.0 %copy-start = (bf16[512,256]{1,0:T(8,128)(2,1)S(1)}, bf16[512,256]{1,0:T(8,128)(2,1)}, u32[]{:S(2)}) copy-start(bf16[512,256]{1,0:T(8,128)(2,1)} %param.8) | copy-start | bytes 786436
  18.6 21.3 %all-to-all-start.1 = ((bf16[16,1,128,256]{3,2,1,0:T(8,128)(2,1)}), bf16[16,1,128,256]{3,2,1,0:T(8,128)(2,1)S(1)}, u32[]{:S(2)}, u32[]{:S(2)}) async-start(bf16[16,1,128,256]{3,2,1,0:T(8,128)(2,1)} %bitcast.7), calls=%async_computation.1 | async-start | bytes 2097152 | tf_op jit(solution)/shard_map/all_to_all | solution.py:89
  62.4 5.2 %copy-start.1 = (s32[1,16,1]{1,2,0:T(1,128)S(1)}, s32[1,16,1]{1,2,0:T(1,128)}, u32[]{:S(2)}) copy-start(s32[1,16,1]{1,2,0:T(1,128)} %param.9) | copy-start | bytes 196
  62.4 31.0 %all-to-all-start.2 = ((f32[8,16,32,128]{3,2,1,0:T(8,128)}), f32[8,16,32,128]{3,2,1,0:T(8,128)S(1)}, u32[]{:S(2)}, u32[]{:S(2)}) async-start(f32[8,16,32,128]{3,2,1,0:T(8,128)} %shard_map.64), calls=%async_computation.2 | async-start | bytes 4194304 | tf_op jit(solution)/shard_map/all_to_all | solution.py:94
  95.1 16.9 %all-to-all-start.3 = ((f32[16,2,32,128]{3,2,1,0:T(8,128)}), f32[16,2,32,128]{3,2,1,0:T(8,128)S(1)}, u32[]{:S(2)}, u32[]{:S(2)}) async-start(f32[16,2,32,128]{3,2,1,0:T(8,128)} %broadcast_select_fusion), calls=%async_computation.3 | async-start | bytes 1048576 | tf_op jit(solution)/shard_map/all_to_all | solution.py:112

commit v6 on v5

--- a/solution.py
+++ b/solution.py
@@ -17,19 +17,21 @@
     tiles, n_p, bs, _ = t_ref.shape
     occ = c_ref.shape[2]
 
-    @pl.when(step == 0)
-    def _():
-        acc[...] = jnp.zeros_like(acc)
-
     for t in range(tiles):
         block = t_ref[t].reshape(n_p * bs, bs)
         half = jnp.dot(block, c_ref[t], preferred_element_type=jnp.float32).astype(jnp.bfloat16)
         for j in range(n_p):
             hbuf[t * bs:(t + 1) * bs, j * occ:(j + 1) * occ] = half[j * bs:(j + 1) * bs]
     for r in range(0, tiles * bs, ROW_CHUNK):
-        acc[r:r + ROW_CHUNK] += jnp.dot(
-            hbuf[r:r + ROW_CHUNK], s_ref[...], preferred_element_type=jnp.float32
-        )
+        term = jnp.dot(hbuf[r:r + ROW_CHUNK], s_ref[...], preferred_element_type=jnp.float32)
+
+        @pl.when(step == 0)
+        def _():
+            acc[r:r + ROW_CHUNK] = term
+
+        @pl.when(step > 0)
+        def _():
+            acc[r:r + ROW_CHUNK] += term
 
     @pl.when(step == pl.num_programs(0) - 1)
     def _():
@@ -77,8 +79,13 @@
     block_ids = tile_block[0]
     lam_ids = tile_lam[0]
 
-    lists = jnp.broadcast_to(jnp.concatenate([owner_ids, block_ids])[None, :], (n_blk, 2 * tiles))
-    ints = jnp.concatenate([lam_ids.reshape(n_blk, per_group), lists], axis=1).astype(jnp.int32)
+    col = lax.broadcasted_iota(jnp.int32, (n_blk, per_group + 2 * tiles), 1)
+    lists = jnp.concatenate([jnp.zeros((per_group,), jnp.int32), owner_ids, block_ids])
+    if per_group == 1:
+        lam_cols = jnp.broadcast_to(lam_ids[:, None], col.shape)
+    else:
+        lam_cols = jnp.pad(lam_ids.reshape(n_blk, per_group), ((0, 0), (0, 2 * tiles)))
+    ints = jnp.where(col < per_group, lam_cols, lists[None, :]).astype(jnp.int32)
     ints_got = lax.all_to_all(ints, "blk", 0, 0, tiled=True)
     lam_req = ints_got[:, :per_group]
     all_owner = ints_got[:, per_group:per_group + tiles]

time: 113 us -> 127 us (1.12)
  Pallas kernels: 22.5 us -> 35.9 us
    pallas_call x1, Pallas kernels: 22.5 us -> 35.9 us  [tile_partials(): pl.pallas_call(tile_kernel, grid=(n_p // P_CHUNK,), in_specs=[pl.BlockSpe...]
  transfers between devices with their start and end apart: 3 -> 3, of which waited for: 3 -> 3; matrix products, arithmetic and copies ran while one was open for 7% -> 6% of each run, Pallas kernels for 0% -> 0%
where the time goes in v6:
time: 127 us; the launch traced here: 126 us
  waiting for transfers between devices  46.1 us (36%)
  Pallas kernels  35.9 us (28%)
  blocking collectives  15.2 us (12%)
  starting transfers between devices  15.1 us (12%)
  local copies, waits for them, and re-layouts  9.09 us (7%)
  other arithmetic  4.7 us (4%)
    pallas_call x1, Pallas kernels, tile_partials(): pl.pallas_call(tile_kernel, grid=(n_p // P_CHUNK,), in_specs=[pl.BlockSpe...  35.9 us
    all_to_all x1, waiting for transfers between devices, local(): reduced = jnp.sum(lax.all_to_all(partial, 'aux', 0, 0, tiled=True), axis=0)  25.2 us
    all_to_all x1, blocking collectives, local(): ints_got = lax.all_to_all(ints, 'blk', 0, 0, tiled=True)  15.2 us
    all_to_all x1, waiting for transfers between devices, local(): lax.all_to_all(send_panels, 'blk', 0, 0, tiled=True).reshape(tiles, bs, occ)  10.8 us
    all_to_all x1, waiting for transfers between devices, local(): received = lax.all_to_all(send_tiles, 'blk', 0, 0, tiled=True)  10.1 us
    transpose x1, local copies, waits for them, and re-layouts, local(): slab_t = jnp.swapaxes(slab_factor, 1, 2).reshape(n_p * occ, slab)  6.42 us
    all_to_all x1, starting transfers between devices, local(): received = lax.all_to_all(send_tiles, 'blk', 0, 0, tiled=True)  5.76 us
    all_to_all x1, starting transfers between devices, local(): reduced = jnp.sum(lax.all_to_all(partial, 'aux', 0, 0, tiled=True), axis=0)  5.23 us
  transfers between devices with their start and end apart: 3, of which 3 were waited for; matrix products, arithmetic and copies ran while one was open for 6% of the time, Pallas kernels for 0%

profile of v6, /device:TPU:1, one launch (start us, length us, event | category | flops | bytes accessed | tf_op | source)
XLA Modules:
  0.0 126.2 jit_solution(4177231496869914309)
XLA Ops:
  0.0 0.0 copy-start
  0.0 0.8 pad_add_fusion
  0.8 0.7 broadcast_select_fusion.1
  1.5 15.2 %all_to_all.24 = s32[16,1,33]{2,1,0:T(1,128)S(1)} all-to-all(s32[16,1,33]{2,1,0:T(1,128)S(1)} %broadcast_select_fusion.1), channel_id=1, replica_groups=mesh['blk'=16,'aux'=8] {'blk'}, dimensions={0} | all-to-all | bytes 4224 | tf_op jit(solution)/shard_map/all_to_all | solution.py:89
  16.8 0.1 fusion.1
  16.9 0.0 copy-done
  16.9 1.6 %gather_fusion = bf16[16,128,256]{2,1,0:T(8,128)(2,1)} fusion(bf16[4,128,256]{2,1,0:T(8,128)(2,1)S(1)} %bitcast.20, s32[1024]{0:T(1024)S(1)} %pad_clamp_fusion.1), kind=kCustom, calls=%fused_computation | custom fusion | bytes 2097216 | tf_op jit(solution)/shard_map/gather | solution.py:95
  18.5 4.1 %all-to-all-start.1 = ((bf16[16,1,128,256]{3,2,1,0:T(8,128)(2,1)}), bf16[16,1,128,256]{3,2,1,0:T(8,128)(2,1)S(1)}, u32[]{:S(2)}, u32[]{:S(2)}) async-start(bf16[16,1,128,256]{3,2,1,0:T(8,128)(2,1)} %bitcast.6), calls=%async_computation.1 | async-start | bytes 2097152 | tf_op jit(solution)/shard_map/all_to_all | solution.py:96
  22.6 6.4 %copy.20 = bf16[32,256,256]{2,1,0:T(8,128)(2,1)} copy(bf16[32,256,256]{1,2,0:T(8,128)(2,1)} %bitcast.22) | data formatting | bytes 8388608 | tf_op jit(solution)/shard_map/transpose | solution.py:99
  29.0 10.8 %all-to-all-done.1 = bf16[16,1,128,256]{3,2,1,0:T(8,128)(2,1)S(1)} async-done(((bf16[16,1,128,256]{3,2,1,0:T(8,128)(2,1)}), bf16[16,1,128,256]{3,2,1,0:T(8,128)(2,1)S(1)}, u32[]{:S(2)}, u32[]{:S(2)}) %all-to-all-start.1) | async-done | bytes 1048608 | tf_op jit(solution)/shard_map/all_to_all | solution.py:96
  39.8 35.9 %shard_map.64 = f32[8,16,32,128]{3,2,1,0:T(8,128)} custom-call(bf16[16,32,128,128]{3,2,1,0:T(8,128)(2,1)} %bitcast.36, bf16[16,128,256]{2,1,0:T(8,128)(2,1)S(1)} %bitcast.21, bf16[8192,256]{1,0:T(8,128)(2,1)} %bitcast.23), custom_call_target="tpu_custom_call" | custom-call | flops 12884901888 | bytes 24117248 | tf_op jit(solution)/shard_map/pallas_call | solution.py:49
  75.7 0.0 copy-start.1
  75.7 5.2 %all-to-all-start.2 = ((f32[8,16,32,128]{3,2,1,0:T(8,128)}), f32[8,16,32,128]{3,2,1,0:T(8,128)S(1)}, u32[]{:S(2)}, u32[]{:S(2)}) async-start(f32[8,16,32,128]{3,2,1,0:T(8,128)} %shard_map.64), calls=%async_computation.2 | async-start | bytes 4194304 | tf_op jit(solution)/shard_map/all_to_all | solution.py:101
  80.9 0.0 copy-done.1
  80.9 0.2 convert_reduce_fusion.1
  81.1 0.1 fusion.2
  81.2 0.1 broadcast_in_dim.103
  81.3 0.1 select_reduce_fusion.5
  81.4 0.1 fusion.4
  81.5 25.2 %all-to-all-done.2 = f32[8,16,32,128]{3,2,1,0:T(8,128)S(1)} async-done(((f32[8,16,32,128]{3,2,1,0:T(8,128)}), f32[8,16,32,128]{3,2,1,0:T(8,128)S(1)}, u32[]{:S(2)}, u32[]{:S(2)}) %all-to-all-start.2) | async-done | bytes 2097184 | tf_op jit(solution)/shard_map/all_to_all | solution.py:101
  106.7 0.2 reduce_sum.86
  106.9 0.6 gather_fusion.1
  107.5 0.9 broadcast_select_fusion
  108.4 5.8 %all-to-all-start.3 = ((f32[16,2,32,128]{3,2,1,0:T(8,128)}), f32[16,2,32,128]{3,2,1,0:T(8,128)S(1)}, u32[]{:S(2)}, u32[]{:S(2)}) async-start(f32[16,2,32,128]{3,2,1,0:T(8,128)} %broadcast_select_fusion), calls=%async_computation.3 | async-start | bytes 1048576 | tf_op jit(solution)/shard_map/all_to_all | solution.py:119
  114.1 0.1 broadcast_compare_fusion
  114.2 0.4 convert_reduce_fusion
  114.6 0.1 select_reduce_fusion.4
  114.8 0.1 copy.19
  114.9 0.1 copy.21
  115.0 0.1 copy.22
  115.1 0.1 copy.23
  115.2 10.1 %all-to-all-done.3 = f32[16,2,32,128]{3,2,1,0:T(8,128)S(1)} async-done(((f32[16,2,32,128]{3,2,1,0:T(8,128)}), f32[16,2,32,128]{3,2,1,0:T(8,128)S(1)}, u32[]{:S(2)}, u32[]{:S(2)}) %all-to-all-start.3) | async-done | bytes 524320 | tf_op jit(solution)/shard_map/all_to_all | solution.py:119
  125.3 0.2 select_reduce_fusion.3
  125.5 0.6 pad_maximum_fusion
  (7 shorter events, 0.1 us)
Async XLA Ops:
  0.0 16.9 %copy-start = (bf16[512,256]{1,0:T(8,128)(2,1)S(1)}, bf16[512,256]{1,0:T(8,128)(2,1)}, u32[]{:S(2)}) copy-start(bf16[512,256]{1,0:T(8,128)(2,1)} %param.8) | copy-start | bytes 786436
  18.5 21.3 %all-to-all-start.1 = ((bf16[16,1,128,256]{3,2,1,0:T(8,128)(2,1)}), bf16[16,1,128,256]{3,2,1,0:T(8,128)(2,1)S(1)}, u32[]{:S(2)}, u32[]{:S(2)}) async-start(bf16[16,1,128,256]{3,2,1,0:T(8,128)(2,1)} %bitcast.6), calls=%async_computation.1 | async-start | bytes 2097152 | tf_op jit(solution)/shard_map/all_to_all | solution.py:96
  75.7 5.2 %copy-start.1 = (s32[1,16,1]{1,2,0:T(1,128)S(1)}, s32[1,16,1]{1,2,0:T(1,128)}, u32[]{:S(2)}) copy-start(s32[1,16,1]{1,2,0:T(1,128)} %param.9) | copy-start | bytes 196
  75.7 31.0 %all-to-all-start.2 = ((f32[8,16,32,128]{3,2,1,0:T(8,128)}), f32[8,16,32,128]{3,2,1,0:T(8,128)S(1)}, u32[]{:S(2)}, u32[]{:S(2)}) async-start(f32[8,16,32,128]{3,2,1,0:T(8,128)} %shard_map.64), calls=%async_computation.2 | async-start | bytes 4194304 | tf_op jit(solution)/shard_map/all_to_all | solution.py:101
  108.4 16.9 %all-to-all-start.3 = ((f32[16,2,32,128]{3,2,1,0:T(8,128)}), f32[16,2,32,128]{3,2,1,0:T(8,128)S(1)}, u32[]{:S(2)}, u32[]{:S(2)}) async-start(f32[16,2,32,128]{3,2,1,0:T(8,128)} %broadcast_select_fusion), calls=%async_computation.3 | async-start | bytes 1048576 | tf_op jit(solution)/shard_map/all_to_all | solution.py:119

commit v7 on v5

--- a/solution.py
+++ b/solution.py
@@ -90,8 +90,12 @@
 
     n_p, slab = slab_factor.shape[0], slab_factor.shape[1]
     slab_t = jnp.swapaxes(slab_factor, 1, 2).reshape(n_p * occ, slab)
-    partial = tile_partials(tile_data, panels, slab_t, n_aux)
-    reduced = jnp.sum(lax.all_to_all(partial, "aux", 0, 0, tiled=True), axis=0)
+    half_tiles = tiles // 2
+    reduced = []
+    for lo in (0, half_tiles):
+        part = tile_partials(tile_data[lo:lo + half_tiles], panels[lo:lo + half_tiles], slab_t, n_aux)
+        reduced.append(jnp.sum(lax.all_to_all(part, "aux", 0, 0, tiled=True), axis=0))
+    reduced = jnp.concatenate(reduced, axis=0)
 
     same_owner = owner_ids[:, None] == owner_ids[None, :]
     earlier = jnp.arange(tiles)[None, :] < jnp.arange(tiles)[:, None]

time: 113 us -> 118 us (1.044)
  waiting for transfers between devices: 46.1 us -> 29.3 us
  starting transfers between devices: 15.1 us -> 31.7 us
  local copies, waits for them, and re-layouts: 9.94 us -> 26.2 us
  blocking collectives: 15.2 us -> 0 us
  Pallas kernels: 22.5 us -> 25.4 us
    all_to_all x1 -> x0, blocking collectives: 15.2 us -> none  [local(): ints_got = lax.all_to_all(ints, 'blk', 0, 0, tiled=True)]
    all_to_all x1 -> x3, starting transfers between devices: 5.23 us -> 18.7 us  [the longest x2 10.2 us: local(): lax.all_to_all(part, 'aux', 0, 0, tiled=True)]
    slice x0 -> x2, local copies, waits for them, and re-layouts: none -> 11.9 us  [the longest x1 11.8 us: local(): tile_data[lo:lo + half_tiles]]
    all_to_all x1 -> x3, waiting for transfers between devices: 25.2 us -> 14 us  [the longest x2 13.5 us: local(): lax.all_to_all(part, 'aux', 0, 0, tiled=True)]
    all_to_all x1, waiting for transfers between devices: 10.8 us -> 5.23 us  [local(): lax.all_to_all(send_panels, 'blk', 0, 0, tiled=True).reshape(tiles, bs, occ)]
    unnamed x4 -> x8, local copies, waits for them, and re-layouts: 0.01 us -> 4.38 us
    pallas_call x1 -> x2, Pallas kernels: 22.5 us -> 25.4 us  [tile_partials(): pl.pallas_call(tile_kernel, grid=(n_p // P_CHUNK,), in_specs=[pl.BlockSpe...]
    all_to_all x1, starting transfers between devices: 4.11 us -> 6.71 us  [local(): lax.all_to_all(send_panels, 'blk', 0, 0, tiled=True).reshape(tiles, bs, occ)]
  transfers between devices with their start and end apart: 3 -> 5, of which waited for: 3 -> 4; matrix products, arithmetic and copies ran while one was open for 7% -> 17% of each run, Pallas kernels for 0% -> 11%
where the time goes in v7:
time: 118 us; the launch traced here: 117 us
  starting transfers between devices  31.7 us (27%)
  waiting for transfers between devices  29.3 us (25%)
  local copies, waits for them, and re-layouts  26.2 us (22%)
  Pallas kernels  25.4 us (22%)
  other arithmetic  4.48 us (4%)
    pallas_call x2, Pallas kernels, tile_partials(): pl.pallas_call(tile_kernel, grid=(n_p // P_CHUNK,), in_specs=[pl.BlockSpe...  25.4 us
    all_to_all x2, waiting for transfers between devices, local(): lax.all_to_all(part, 'aux', 0, 0, tiled=True)  13.5 us
    slice x1, local copies, waits for them, and re-layouts, local(): tile_data[lo:lo + half_tiles]  11.8 us
    all_to_all x2, starting transfers between devices, local(): lax.all_to_all(part, 'aux', 0, 0, tiled=True)  10.2 us
    all_to_all x1, waiting for transfers between devices, local(): received = lax.all_to_all(send_tiles, 'blk', 0, 0, tiled=True)  10.1 us
    all_to_all x1, starting transfers between devices, local(): ints_got = lax.all_to_all(ints, 'blk', 0, 0, tiled=True)  8.44 us
    all_to_all x1, starting transfers between devices, local(): lax.all_to_all(send_panels, 'blk', 0, 0, tiled=True).reshape(tiles, bs, occ)  6.71 us
    transpose x1, local copies, waits for them, and re-layouts, local(): slab_t = jnp.swapaxes(slab_factor, 1, 2).reshape(n_p * occ, slab)  6.42 us
  transfers between devices with their start and end apart: 5, of which 4 were waited for; matrix products, arithmetic and copies ran while one was open for 17% of the time, Pallas kernels for 11%

profile of v7, /device:TPU:1, one launch (start us, length us, event | category | flops | bytes accessed | tf_op | source)
XLA Modules:
  0.0 117.2 jit_solution(17897621343657652061)
XLA Ops:
  0.0 0.0 copy-start
  0.0 0.8 copy.25
  0.8 0.7 pad_add_fusion.1
  1.5 0.1 pad.7.clone
  1.6 0.6 pad_add_fusion
  2.2 8.4 %all-to-all-start = ((s32[16,1,33]{2,1,0:T(1,128)}), s32[16,1,33]{2,1,0:T(1,128)S(1)}, u32[]{:S(2)}, u32[]{:S(2)}) async-start(s32[16,1,33]{2,1,0:T(1,128)} %bitcast.3), calls=%async_computation | async-start | bytes 16384 | tf_op jit(solution)/shard_map/all_to_all | solution.py:82
  10.6 6.4 %copy.28 = bf16[32,256,256]{2,1,0:T(8,128)(2,1)} copy(bf16[32,256,256]{1,2,0:T(8,128)(2,1)} %bitcast.31) | data formatting | bytes 8388608 | tf_op jit(solution)/shard_map/transpose | solution.py:92
  17.1 0.5 all-to-all-done
  17.6 0.1 fusion.1
  17.7 0.0 copy-done
  17.7 1.6 %gather_fusion = bf16[16,128,256]{2,1,0:T(8,128)(2,1)} fusion(bf16[4,128,256]{2,1,0:T(8,128)(2,1)S(1)} %bitcast.28, s32[1024]{0:T(1024)S(1)} %pad_clamp_fusion.1), kind=kCustom, calls=%fused_computation | custom fusion | bytes 2097216 | tf_op jit(solution)/shard_map/gather | solution.py:88
  19.3 6.7 %all-to-all-start.1 = ((bf16[16,1,128,256]{3,2,1,0:T(8,128)(2,1)}), bf16[16,1,128,256]{3,2,1,0:T(8,128)(2,1)S(1)}, u32[]{:S(2)}, u32[]{:S(2)}) async-start(bf16[16,1,128,256]{3,2,1,0:T(8,128)(2,1)} %bitcast.7), calls=%async_computation.1 | async-start | bytes 2097152 | tf_op jit(solution)/shard_map/all_to_all | solution.py:89
  26.0 11.8 %slice_bitcast_fusion.1 = (bf16[8,32,128,128]{3,2,1,0:T(8,128)(2,1)}, bf16[8,32,128,128]{3,2,1,0:T(8,128)(2,1)}) fusion(bf16[1,16,32,128,128]{4,3,2,1,0:T(8,128)(2,1)} %param.6), kind=kLoop, calls=%fused_computation.3 | loop fusion | bytes 33554432 | tf_op jit(solution)/shard_map/slice | solution.py:96
  37.9 5.2 %all-to-all-done.1 = bf16[16,1,128,256]{3,2,1,0:T(8,128)(2,1)S(1)} async-done(((bf16[16,1,128,256]{3,2,1,0:T(8,128)(2,1)}), bf16[16,1,128,256]{3,2,1,0:T(8,128)(2,1)S(1)}, u32[]{:S(2)}, u32[]{:S(2)}) %all-to-all-start.1) | async-done | bytes 1048608 | tf_op jit(solution)/shard_map/all_to_all | solution.py:89
  43.1 0.1 slice_bitcast_fusion.3
  43.2 0.0 copy-start.1
  43.2 2.2 %copy-done.1 = bf16[32,256,256]{2,1,0:T(8,128)(2,1)S(1)} copy-done((bf16[32,256,256]{2,1,0:T(8,128)(2,1)S(1)}, bf16[32,256,256]{2,1,0:T(8,128)(2,1)}, u32[]{:S(2)}) %copy-start.1) | copy-done | bytes 4194328
  45.4 0.0 copy-start.3
  45.4 12.7 %shard_map.64 = f32[8,8,32,128]{3,2,1,0:T(8,128)} custom-call(bf16[8,32,128,128]{3,2,1,0:T(8,128)(2,1)} %get-tuple-element.9.t_ref, bf16[8,128,256]{2,1,0:T(8,128)(2,1)S(1)} %get-tuple-element.11.c_ref, bf16[8192,256]{1,0:T(8,128)(2,1)S(1)} %bitcast.29), custom_call_target="tpu_custom_call" | custom-call | flops 6442450944 | bytes 14155776 | tf_op jit(solution)/shard_map/pallas_call | solution.py:47
  58.0 5.1 %all-to-all-start.2 = ((f32[8,8,32,128]{3,2,1,0:T(8,128)}), f32[8,8,32,128]{3,2,1,0:T(8,128)S(1)}, u32[]{:S(2)}, u32[]{:S(2)}) async-start(f32[8,8,32,128]{3,2,1,0:T(8,128)} %shard_map.64), calls=%async_computation.2 | async-start | bytes 2097152 | tf_op jit(solution)/shard_map/all_to_all | solution.py:97
  63.1 0.0 copy-done.3
  63.1 0.2 convert_reduce_fusion.1
  63.3 0.0 copy-start.2
  63.3 2.2 %copy-done.2 = bf16[32,256,256]{2,1,0:T(8,128)(2,1)S(1)} copy-done((bf16[32,256,256]{2,1,0:T(8,128)(2,1)S(1)}, bf16[32,256,256]{2,1,0:T(8,128)(2,1)}, u32[]{:S(2)}) %copy-start.2) | copy-done | bytes 4194328
  65.5 12.7 %shard_map.65 = f32[8,8,32,128]{3,2,1,0:T(8,128)} custom-call(bf16[8,32,128,128]{3,2,1,0:T(8,128)(2,1)} %get-tuple-element.10.t_ref, bf16[8,128,256]{2,1,0:T(8,128)(2,1)S(1)} %get-tuple-element.12.c_ref, bf16[8192,256]{1,0:T(8,128)(2,1)S(1)} %bitcast.30), custom_call_target="tpu_custom_call" | custom-call | flops 6442450944 | bytes 14155776 | tf_op jit(solution)/shard_map/pallas_call | solution.py:47
  78.2 0.0 all-to-all-done.2
  78.2 5.1 %all-to-all-start.3 = ((f32[8,8,32,128]{3,2,1,0:T(8,128)}), f32[8,8,32,128]{3,2,1,0:T(8,128)S(1)}, u32[]{:S(2)}, u32[]{:S(2)}) async-start(f32[8,8,32,128]{3,2,1,0:T(8,128)} %shard_map.65), calls=%async_computation.3 | async-start | bytes 2097152 | tf_op jit(solution)/shard_map/all_to_all | solution.py:97
  83.4 0.1 fusion.2
  83.5 0.1 broadcast_in_dim.91
  83.6 0.1 select_reduce_fusion.5
  83.7 0.1 fusion.4
  83.8 0.1 reduce_sum.95
  83.8 13.5 %all-to-all-done.3 = f32[8,8,32,128]{3,2,1,0:T(8,128)S(1)} async-done(((f32[8,8,32,128]{3,2,1,0:T(8,128)}), f32[8,8,32,128]{3,2,1,0:T(8,128)S(1)}, u32[]{:S(2)}, u32[]{:S(2)}) %all-to-all-start.3) | async-done | bytes 1048608 | tf_op jit(solution)/shard_map/all_to_all | solution.py:97
  97.3 0.1 reduce_sum.96
  97.4 0.6 gather_fusion.1
  98.0 0.9 broadcast_select_fusion
  98.9 6.3 %all-to-all-start.4 = ((f32[16,2,32,128]{3,2,1,0:T(8,128)}), f32[16,2,32,128]{3,2,1,0:T(8,128)S(1)}, u32[]{:S(2)}, u32[]{:S(2)}) async-start(f32[16,2,32,128]{3,2,1,0:T(8,128)} %broadcast_select_fusion), calls=%async_computation.4 | async-start | bytes 1048576 | tf_op jit(solution)/shard_map/all_to_all | solution.py:116
  105.2 0.1 broadcast_compare_fusion
  105.3 0.4 convert_reduce_fusion
  105.7 0.1 select_reduce_fusion.4
  105.8 0.1 copy.26
  105.9 0.1 copy.30
  106.0 0.1 copy.31
  106.1 0.1 copy.32
  106.2 10.1 %all-to-all-done.4 = f32[16,2,32,128]{3,2,1,0:T(8,128)S(1)} async-done(((f32[16,2,32,128]{3,2,1,0:T(8,128)}), f32[16,2,32,128]{3,2,1,0:T(8,128)S(1)}, u32[]{:S(2)}, u32[]{:S(2)}) %all-to-all-start.4) | async-done | bytes 524320 | tf_op jit(solution)/shard_map/all_to_all | solution.py:116
  116.4 0.2 select_reduce_fusion.3
  116.6 0.6 pad_maximum_fusion.1
  (7 shorter events, 0.1 us)
Async XLA Ops:
  0.0 17.7 %copy-start = (bf16[512,256]{1,0:T(8,128)(2,1)S(1)}, bf16[512,256]{1,0:T(8,128)(2,1)}, u32[]{:S(2)}) copy-start(bf16[512,256]{1,0:T(8,128)(2,1)} %param.8) | copy-start | bytes 786436
  2.2 15.4 %all-to-all-start = ((s32[16,1,33]{2,1,0:T(1,128)}), s32[16,1,33]{2,1,0:T(1,128)S(1)}, u32[]{:S(2)}, u32[]{:S(2)}) async-start(s32[16,1,33]{2,1,0:T(1,128)} %bitcast.3), calls=%async_computation | async-start | bytes 16384 | tf_op jit(solution)/shard_map/all_to_all | solution.py:82
  19.3 23.8 %all-to-all-start.1 = ((bf16[16,1,128,256]{3,2,1,0:T(8,128)(2,1)}), bf16[16,1,128,256]{3,2,1,0:T(8,128)(2,1)S(1)}, u32[]{:S(2)}, u32[]{:S(2)}) async-start(bf16[16,1,128,256]{3,2,1,0:T(8,128)(2,1)} %bitcast.7), calls=%async_computation.1 | async-start | bytes 2097152 | tf_op jit(solution)/shard_map/all_to_all | solution.py:89
  43.2 2.2 %copy-start.1 = (bf16[32,256,256]{2,1,0:T(8,128)(2,1)S(1)}, bf16[32,256,256]{2,1,0:T(8,128)(2,1)}, u32[]{:S(2)}) copy-start(bf16[32,256,256]{2,1,0:T(8,128)(2,1)} %copy.28) | copy-start | bytes 12582916
  45.4 17.7 %copy-start.3 = (s32[1,16,1]{1,2,0:T(1,128)S(1)}, s32[1,16,1]{1,2,0:T(1,128)}, u32[]{:S(2)}) copy-start(s32[1,16,1]{1,2,0:T(1,128)} %param.9) | copy-start | bytes 196
  58.0 20.2 %all-to-all-start.2 = ((f32[8,8,32,128]{3,2,1,0:T(8,128)}), f32[8,8,32,128]{3,2,1,0:T(8,128)S(1)}, u32[]{:S(2)}, u32[]{:S(2)}) async-start(f32[8,8,32,128]{3,2,1,0:T(8,128)} %shard_map.64), calls=%async_computation.2 | async-start | bytes 2097152 | tf_op jit(solution)/shard_map/all_to_all | solution.py:97
  63.3 2.2 %copy-start.2 = (bf16[32,256,256]{2,1,0:T(8,128)(2,1)S(1)}, bf16[32,256,256]{2,1,0:T(8,128)(2,1)}, u32[]{:S(2)}) copy-start(bf16[32,256,256]{2,1,0:T(8,128)(2,1)} %copy.28) | copy-start | bytes 12582916
  78.2 19.1 %all-to-all-start.3 = ((f32[8,8,32,128]{3,2,1,0:T(8,128)}), f32[8,8,32,128]{3,2,1,0:T(8,128)S(1)}, u32[]{:S(2)}, u32[]{:S(2)}) async-start(f32[8,8,32,128]{3,2,1,0:T(8,128)} %shard_map.65), calls=%async_computation.3 | async-start | bytes 2097152 | tf_op jit(solution)/shard_map/all_to_all | solution.py:97
  98.9 17.5 %all-to-all-start.4 = ((f32[16,2,32,128]{3,2,1,0:T(8,128)}), f32[16,2,32,128]{3,2,1,0:T(8,128)S(1)}, u32[]{:S(2)}, u32[]{:S(2)}) async-start(f32[16,2,32,128]{3,2,1,0:T(8,128)} %broadcast_select_fusion), calls=%async_computation.4 | async-start | bytes 1048576 | tf_op jit(solution)/shard_map/all_to_all | solution.py:116

commit v8 on v5

--- a/solution.py
+++ b/solution.py
@@ -85,7 +85,10 @@
     all_block = ints_got[:, per_group + tiles:]
 
     coef_blocks = coefficients.reshape(blocks_dev, bs, occ)
-    send_panels = coef_blocks[lam_req.reshape(-1)].reshape(n_blk, per_group, bs, occ)
+    lam_sel = lam_req[:, :, None, None]
+    send_panels = jnp.broadcast_to(coef_blocks[0], (n_blk, per_group, bs, occ))
+    for b in range(1, blocks_dev):
+        send_panels = jnp.where(lam_sel == b, coef_blocks[b][None, None], send_panels)
     panels = lax.all_to_all(send_panels, "blk", 0, 0, tiled=True).reshape(tiles, bs, occ)
 
     n_p, slab = slab_factor.shape[0], slab_factor.shape[1]

time: 113 us -> 114 us (level)
  blocking collectives: 15.2 us -> 0 us
  starting transfers between devices: 15.1 us -> 23.5 us
  waiting for transfers between devices: 46.1 us -> 52.1 us
  other arithmetic: 3.93 us -> 5.82 us
    all_to_all x1 -> x0, blocking collectives: 15.2 us -> none  [local(): ints_got = lax.all_to_all(ints, 'blk', 0, 0, tiled=True)]
    all_to_all x0 -> x1, starting transfers between devices: none -> 8.44 us  [local(): ints_got = lax.all_to_all(ints, 'blk', 0, 0, tiled=True)]
    all_to_all x0 -> x1, waiting for transfers between devices: none -> 5.99 us  [local(): ints_got = lax.all_to_all(ints, 'blk', 0, 0, tiled=True)]
    gather x1 -> x0, local copies, waits for them, and re-layouts: 1.59 us -> none  [local(): coef_blocks[lam_req.reshape(-1)].reshape(n_blk, per_group, bs, occ)]
    select_n x1, other arithmetic: 0.11 us -> 1.27 us  [local(): jnp.where(lam_sel == b, coef_blocks[b][None, None], send_panels)]
  transfers between devices with their start and end apart: 3 -> 4, of which waited for: 3 -> 4; matrix products, arithmetic and copies ran while one was open for 7% -> 8% of each run, Pallas kernels for 0% -> 0%
where the time goes in v8:
time: 114 us; the launch traced here: 113 us
  waiting for transfers between devices  52.1 us (46%)
  starting transfers between devices  23.5 us (21%)
  Pallas kernels  22.5 us (20%)
  local copies, waits for them, and re-layouts  9.25 us (8%)
  other arithmetic  5.82 us (5%)
    all_to_all x1, waiting for transfers between devices, local(): reduced = jnp.sum(lax.all_to_all(partial, 'aux', 0, 0, tiled=True), axis=0)  25.2 us
    pallas_call x1, Pallas kernels, tile_partials(): pl.pallas_call(tile_kernel, grid=(n_p // P_CHUNK,), in_specs=[pl.BlockSpe...  22.5 us
    all_to_all x1, waiting for transfers between devices, local(): lax.all_to_all(send_panels, 'blk', 0, 0, tiled=True).reshape(tiles, bs, occ)  10.8 us
    all_to_all x1, waiting for transfers between devices, local(): received = lax.all_to_all(send_tiles, 'blk', 0, 0, tiled=True)  10.1 us
    all_to_all x1, starting transfers between devices, local(): ints_got = lax.all_to_all(ints, 'blk', 0, 0, tiled=True)  8.44 us
    transpose x1, local copies, waits for them, and re-layouts, local(): slab_t = jnp.swapaxes(slab_factor, 1, 2).reshape(n_p * occ, slab)  6.42 us
    all_to_all x1, waiting for transfers between devices, local(): ints_got = lax.all_to_all(ints, 'blk', 0, 0, tiled=True)  5.99 us
    all_to_all x1, starting transfers between devices, local(): received = lax.all_to_all(send_tiles, 'blk', 0, 0, tiled=True)  5.75 us
  transfers between devices with their start and end apart: 4, of which 4 were waited for; matrix products, arithmetic and copies ran while one was open for 8% of the time, Pallas kernels for 0%

profile of v8, /device:TPU:1, one launch (start us, length us, event | category | flops | bytes accessed | tf_op | source)
XLA Modules:
  0.0 113.3 jit_solution(8799478484513557381)
XLA Ops:
  0.0 0.7 copy.21
  0.7 0.7 pad_add_fusion.1
  1.5 0.1 pad.5.clone
  1.6 0.6 pad_add_fusion
  2.2 8.4 %all-to-all-start = ((s32[16,1,33]{2,1,0:T(1,128)}), s32[16,1,33]{2,1,0:T(1,128)S(1)}, u32[]{:S(2)}, u32[]{:S(2)}) async-start(s32[16,1,33]{2,1,0:T(1,128)} %bitcast.3), calls=%async_computation | async-start | bytes 16384 | tf_op jit(solution)/shard_map/all_to_all | solution.py:82
  10.6 1.0 fusion.3
  11.6 6.0 %all-to-all-done = s32[16,1,33]{2,1,0:T(1,128)S(1)} async-done(((s32[16,1,33]{2,1,0:T(1,128)}), s32[16,1,33]{2,1,0:T(1,128)S(1)}, u32[]{:S(2)}, u32[]{:S(2)}) %all-to-all-start) | async-done | bytes 2144 | tf_op jit(solution)/shard_map/all_to_all | solution.py:82
  17.5 0.1 compare_reduce_fusion.2
  17.7 1.3 %select_select_fusion = bf16[16,1,128,256]{3,2,1,0:T(8,128)(2,1)} fusion(pred[16]{0:T(512)(128)(4,1)S(1)} %get-tuple-element.11, pred[16]{0:T(512)(128)(4,1)S(1)} %get-tuple-element.10, pred[16]{0:T(512)(128)(4,1)S(1)} %get-tuple-element.9, bf16[128,256]{1,0:T(8,128)(2,1)S(1)} %get-tuple-element.14, bf16[128,256]{1,0:T(8,128)(2,1)S(1)} %get-tuple-element.15, ...), kind=kLoop, calls=%fused_computation.1 | loop fusion | flops 1572864 | bytes 1310768 | tf_op jit(solution)/shard_map/jit(_where)/select_n | solution.py:91
  19.0 4.1 %all-to-all-start.1 = ((bf16[16,1,128,256]{3,2,1,0:T(8,128)(2,1)}), bf16[16,1,128,256]{3,2,1,0:T(8,128)(2,1)S(1)}, u32[]{:S(2)}, u32[]{:S(2)}) async-start(bf16[16,1,128,256]{3,2,1,0:T(8,128)(2,1)} %select_select_fusion), calls=%async_computation.1 | async-start | bytes 2097152 | tf_op jit(solution)/shard_map/all_to_all | solution.py:92
  23.1 6.4 %copy.23 = bf16[32,256,256]{2,1,0:T(8,128)(2,1)} copy(bf16[32,256,256]{1,2,0:T(8,128)(2,1)} %bitcast.20) | data formatting | bytes 8388608 | tf_op jit(solution)/shard_map/transpose | solution.py:95
  29.5 10.8 %all-to-all-done.1 = bf16[16,1,128,256]{3,2,1,0:T(8,128)(2,1)S(1)} async-done(((bf16[16,1,128,256]{3,2,1,0:T(8,128)(2,1)}), bf16[16,1,128,256]{3,2,1,0:T(8,128)(2,1)S(1)}, u32[]{:S(2)}, u32[]{:S(2)}) %all-to-all-start.1) | async-done | bytes 1048608 | tf_op jit(solution)/shard_map/all_to_all | solution.py:92
  40.2 22.5 %shard_map.64 = f32[8,16,32,128]{3,2,1,0:T(8,128)} custom-call(bf16[16,32,128,128]{3,2,1,0:T(8,128)(2,1)} %bitcast.31, bf16[16,128,256]{2,1,0:T(8,128)(2,1)S(1)} %bitcast.19, bf16[8192,256]{1,0:T(8,128)(2,1)} %bitcast.21), custom_call_target="tpu_custom_call" | custom-call | flops 12884901888 | bytes 24117248 | tf_op jit(solution)/shard_map/pallas_call | solution.py:47
  62.8 0.0 copy-start
  62.8 5.2 %all-to-all-start.2 = ((f32[8,16,32,128]{3,2,1,0:T(8,128)}), f32[8,16,32,128]{3,2,1,0:T(8,128)S(1)}, u32[]{:S(2)}, u32[]{:S(2)}) async-start(f32[8,16,32,128]{3,2,1,0:T(8,128)} %shard_map.64), calls=%async_computation.2 | async-start | bytes 4194304 | tf_op jit(solution)/shard_map/all_to_all | solution.py:97
  68.0 0.0 copy-done
  68.0 0.2 convert_reduce_fusion.1
  68.2 0.1 fusion.1
  68.3 0.1 broadcast_in_dim.130
  68.4 0.1 select_reduce_fusion.5
  68.5 0.1 fusion.4
  68.6 25.2 %all-to-all-done.2 = f32[8,16,32,128]{3,2,1,0:T(8,128)S(1)} async-done(((f32[8,16,32,128]{3,2,1,0:T(8,128)}), f32[8,16,32,128]{3,2,1,0:T(8,128)S(1)}, u32[]{:S(2)}, u32[]{:S(2)}) %all-to-all-start.2) | async-done | bytes 2097184 | tf_op jit(solution)/shard_map/all_to_all | solution.py:97
  93.8 0.2 reduce_sum.86
  94.0 0.6 gather_fusion
  94.6 0.9 broadcast_select_fusion
  95.5 5.8 %all-to-all-start.3 = ((f32[16,2,32,128]{3,2,1,0:T(8,128)}), f32[16,2,32,128]{3,2,1,0:T(8,128)S(1)}, u32[]{:S(2)}, u32[]{:S(2)}) async-start(f32[16,2,32,128]{3,2,1,0:T(8,128)} %broadcast_select_fusion), calls=%async_computation.3 | async-start | bytes 1048576 | tf_op jit(solution)/shard_map/all_to_all | solution.py:115
  101.2 0.1 broadcast_compare_fusion
  101.3 0.4 convert_reduce_fusion
  101.7 0.1 select_reduce_fusion.4
  101.9 0.1 copy.22
  102.0 0.1 copy.24
  102.1 0.1 copy.25
  102.2 0.1 copy.26
  102.3 10.1 %all-to-all-done.3 = f32[16,2,32,128]{3,2,1,0:T(8,128)S(1)} async-done(((f32[16,2,32,128]{3,2,1,0:T(8,128)}), f32[16,2,32,128]{3,2,1,0:T(8,128)S(1)}, u32[]{:S(2)}, u32[]{:S(2)}) %all-to-all-start.3) | async-done | bytes 524320 | tf_op jit(solution)/shard_map/all_to_all | solution.py:115
  112.4 0.2 select_reduce_fusion.3
  112.6 0.6 pad_maximum_fusion
  (5 shorter events, 0.0 us)
Async XLA Ops:
  2.2 15.4 %all-to-all-start = ((s32[16,1,33]{2,1,0:T(1,128)}), s32[16,1,33]{2,1,0:T(1,128)S(1)}, u32[]{:S(2)}, u32[]{:S(2)}) async-start(s32[16,1,33]{2,1,0:T(1,128)} %bitcast.3), calls=%async_computation | async-start | bytes 16384 | tf_op jit(solution)/shard_map/all_to_all | solution.py:82
  19.0 21.3 %all-to-all-start.1 = ((bf16[16,1,128,256]{3,2,1,0:T(8,128)(2,1)}), bf16[16,1,128,256]{3,2,1,0:T(8,128)(2,1)S(1)}, u32[]{:S(2)}, u32[]{:S(2)}) async-start(bf16[16,1,128,256]{3,2,1,0:T(8,128)(2,1)} %select_select_fusion), calls=%async_computation.1 | async-start | bytes 2097152 | tf_op jit(solution)/shard_map/all_to_all | solution.py:92
  62.8 5.2 %copy-start = (s32[1,16,1]{1,2,0:T(1,128)S(1)}, s32[1,16,1]{1,2,0:T(1,128)}, u32[]{:S(2)}) copy-start(s32[1,16,1]{1,2,0:T(1,128)} %param.9) | copy-start | bytes 196
  62.8 31.0 %all-to-all-start.2 = ((f32[8,16,32,128]{3,2,1,0:T(8,128)}), f32[8,16,32,128]{3,2,1,0:T(8,128)S(1)}, u32[]{:S(2)}, u32[]{:S(2)}) async-start(f32[8,16,32,128]{3,2,1,0:T(8,128)} %shard_map.64), calls=%async_computation.2 | async-start | bytes 4194304 | tf_op jit(solution)/shard_map/all_to_all | solution.py:97
  95.5 16.9 %all-to-all-start.3 = ((f32[16,2,32,128]{3,2,1,0:T(8,128)}), f32[16,2,32,128]{3,2,1,0:T(8,128)S(1)}, u32[]{:S(2)}, u32[]{:S(2)}) async-start(f32[16,2,32,128]{3,2,1,0:T(8,128)} %broadcast_select_fusion), calls=%async_computation.3 | async-start | bytes 1048576 | tf_op jit(solution)/shard_map/all_to_all | solution.py:115

commit v9 on v5

--- a/solution.py
+++ b/solution.py
@@ -106,8 +106,8 @@
     mine = (all_owner == me)[:, None, :] & (all_rank[:, None, :] == jnp.arange(CAP)[None, :, None])
     labels = (jnp.sum(jnp.where(mine, all_block[:, None, :] + 1, 0), axis=2) - 1).reshape(-1)
 
-    picked = reduced[slot_tile]
-    send_tiles = jnp.where(slot_valid[:, None, None], picked, 0.0)
+    with_zero = jnp.concatenate([reduced, jnp.zeros((1,) + reduced.shape[1:], reduced.dtype)], axis=0)
+    send_tiles = with_zero[jnp.where(slot_valid, slot_tile, tiles)]
     send_tiles = send_tiles.reshape((n_blk, CAP) + send_tiles.shape[1:])
     received = lax.all_to_all(send_tiles, "blk", 0, 0, tiled=True)
     received = received.reshape((n_blk * CAP,) + received.shape[2:])

time: 113 us -> 113 us (level)
  no operation moved by 1% of the time
where the time goes in v9:
time: 113 us
  waiting for transfers between devices  46.2 us (41%)
  Pallas kernels  22.5 us (20%)
  blocking collectives  15.2 us (13%)
  starting transfers between devices  15.1 us (13%)
  local copies, waits for them, and re-layouts  10.7 us (9%)
  other arithmetic  3.03 us (3%)
    all_to_all x1, waiting for transfers between devices, local(): reduced = jnp.sum(lax.all_to_all(partial, 'aux', 0, 0, tiled=True), axis=0)  25.3 us
    pallas_call x1, Pallas kernels, tile_partials(): pl.pallas_call(tile_kernel, grid=(n_p // P_CHUNK,), in_specs=[pl.BlockSpe...  22.5 us
    all_to_all x1, blocking collectives, local(): ints_got = lax.all_to_all(ints, 'blk', 0, 0, tiled=True)  15.2 us
    all_to_all x1, waiting for transfers between devices, local(): lax.all_to_all(send_panels, 'blk', 0, 0, tiled=True).reshape(tiles, bs, occ)  10.8 us
    all_to_all x1, waiting for transfers between devices, local(): received = lax.all_to_all(send_tiles, 'blk', 0, 0, tiled=True)  10.1 us
    transpose x1, local copies, waits for them, and re-layouts, local(): slab_t = jnp.swapaxes(slab_factor, 1, 2).reshape(n_p * occ, slab)  6.42 us
    all_to_all x1, starting transfers between devices, local(): received = lax.all_to_all(send_tiles, 'blk', 0, 0, tiled=True)  5.77 us
    all_to_all x1, starting transfers between devices, local(): reduced = jnp.sum(lax.all_to_all(partial, 'aux', 0, 0, tiled=True), axis=0)  5.23 us
  transfers between devices with their start and end apart: 3, of which 3 were waited for; matrix products, arithmetic and copies ran while one was open for 7% of the time, Pallas kernels for 0%

profile of v9, /device:TPU:1, one launch (start us, length us, event | category | flops | bytes accessed | tf_op | source)
XLA Modules:
  0.0 112.8 jit_solution(14220328402553907913)
XLA Ops:
  0.0 0.0 copy-start
  0.0 0.8 copy.16
  0.8 0.7 pad_add_fusion.1
  1.5 0.1 pad.6.clone
  1.6 15.2 %all_to_all.27 = s32[16,1,33]{2,1,0:T(1,128)S(1)} all-to-all(s32[16,1,33]{2,1,0:T(1,128)S(1)} %bitcast.32), channel_id=1, replica_groups=mesh['blk'=16,'aux'=8] {'blk'}, dimensions={0} | all-to-all | bytes 4224 | tf_op jit(solution)/shard_map/all_to_all | solution.py:82
  16.8 0.1 fusion.1
  17.0 0.0 copy-done
  17.0 1.6 %gather_fusion = bf16[16,128,256]{2,1,0:T(8,128)(2,1)} fusion(bf16[4,128,256]{2,1,0:T(8,128)(2,1)S(1)} %bitcast.21, s32[1024]{0:T(1024)S(1)} %pad_clamp_fusion.1), kind=kCustom, calls=%fused_computation | custom fusion | bytes 2097216 | tf_op jit(solution)/shard_map/gather | solution.py:88
  18.6 4.1 %all-to-all-start.1 = ((bf16[16,1,128,256]{3,2,1,0:T(8,128)(2,1)}), bf16[16,1,128,256]{3,2,1,0:T(8,128)(2,1)S(1)}, u32[]{:S(2)}, u32[]{:S(2)}) async-start(bf16[16,1,128,256]{3,2,1,0:T(8,128)(2,1)} %bitcast.7), calls=%async_computation.1 | async-start | bytes 2097152 | tf_op jit(solution)/shard_map/all_to_all | solution.py:89
  22.7 6.4 %copy.18 = bf16[32,256,256]{2,1,0:T(8,128)(2,1)} copy(bf16[32,256,256]{1,2,0:T(8,128)(2,1)} %bitcast.23) | data formatting | bytes 8388608 | tf_op jit(solution)/shard_map/transpose | solution.py:92
  29.1 10.8 %all-to-all-done.1 = bf16[16,1,128,256]{3,2,1,0:T(8,128)(2,1)S(1)} async-done(((bf16[16,1,128,256]{3,2,1,0:T(8,128)(2,1)}), bf16[16,1,128,256]{3,2,1,0:T(8,128)(2,1)S(1)}, u32[]{:S(2)}, u32[]{:S(2)}) %all-to-all-start.1) | async-done | bytes 1048608 | tf_op jit(solution)/shard_map/all_to_all | solution.py:89
  39.8 22.5 %shard_map.64 = f32[8,16,32,128]{3,2,1,0:T(8,128)} custom-call(bf16[16,32,128,128]{3,2,1,0:T(8,128)(2,1)} %bitcast.34, bf16[16,128,256]{2,1,0:T(8,128)(2,1)S(1)} %bitcast.22, bf16[8192,256]{1,0:T(8,128)(2,1)} %bitcast.24), custom_call_target="tpu_custom_call" | custom-call | flops 12884901888 | bytes 24117248 | tf_op jit(solution)/shard_map/pallas_call | solution.py:47
  62.4 0.0 copy-start.1
  62.4 5.2 %all-to-all-start.2 = ((f32[8,16,32,128]{3,2,1,0:T(8,128)}), f32[8,16,32,128]{3,2,1,0:T(8,128)S(1)}, u32[]{:S(2)}, u32[]{:S(2)}) async-start(f32[8,16,32,128]{3,2,1,0:T(8,128)} %shard_map.64), calls=%async_computation.2 | async-start | bytes 4194304 | tf_op jit(solution)/shard_map/all_to_all | solution.py:94
  67.6 0.0 copy-done.1
  67.6 0.2 convert_reduce_fusion.1
  67.8 0.1 fusion.2
  67.9 0.1 select_reduce_fusion.5
  68.0 0.1 fusion.4
  68.1 25.3 %all-to-all-done.2 = f32[8,16,32,128]{3,2,1,0:T(8,128)S(1)} async-done(((f32[8,16,32,128]{3,2,1,0:T(8,128)}), f32[8,16,32,128]{3,2,1,0:T(8,128)S(1)}, u32[]{:S(2)}, u32[]{:S(2)}) %all-to-all-start.2) | async-done | bytes 2097184 | tf_op jit(solution)/shard_map/all_to_all | solution.py:94
  93.4 0.2 reduce_sum.83
  93.6 1.4 %gather_fusion.1 = f32[32,32,128]{2,1,0:T(8,128)} fusion(f32[17,32,128]{2,1,0:T(8,128)S(1)} %concatenate.11, s32[1024]{0:T(1024)S(1)} %pad_clamp_fusion), kind=kCustom, calls=%fused_computation.1 | custom fusion | bytes 1048704 | tf_op jit(solution)/shard_map/gather | solution.py:110
  95.0 5.8 %all-to-all-start.3 = ((f32[16,2,32,128]{3,2,1,0:T(8,128)}), f32[16,2,32,128]{3,2,1,0:T(8,128)S(1)}, u32[]{:S(2)}, u32[]{:S(2)}) async-start(f32[16,2,32,128]{3,2,1,0:T(8,128)} %bitcast.13), calls=%async_computation.3 | async-start | bytes 1048576 | tf_op jit(solution)/shard_map/all_to_all | solution.py:112
  100.8 0.1 broadcast_compare_fusion
  100.8 0.4 convert_reduce_fusion
  101.3 0.1 select_reduce_fusion.4
  101.4 0.1 copy.17
  101.5 0.1 copy.21
  101.6 0.1 copy.20
  101.7 0.1 copy.19
  101.8 10.1 %all-to-all-done.3 = f32[16,2,32,128]{3,2,1,0:T(8,128)S(1)} async-done(((f32[16,2,32,128]{3,2,1,0:T(8,128)}), f32[16,2,32,128]{3,2,1,0:T(8,128)S(1)}, u32[]{:S(2)}, u32[]{:S(2)}) %all-to-all-start.3) | async-done | bytes 524320 | tf_op jit(solution)/shard_map/all_to_all | solution.py:112
  111.9 0.2 select_reduce_fusion.3
  112.1 0.6 pad_maximum_fusion
  (8 shorter events, 0.1 us)
Async XLA Ops:
  0.0 17.0 %copy-start = (bf16[512,256]{1,0:T(8,128)(2,1)S(1)}, bf16[512,256]{1,0:T(8,128)(2,1)}, u32[]{:S(2)}) copy-start(bf16[512,256]{1,0:T(8,128)(2,1)} %param.8) | copy-start | bytes 786436
  18.6 21.3 %all-to-all-start.1 = ((bf16[16,1,128,256]{3,2,1,0:T(8,128)(2,1)}), bf16[16,1,128,256]{3,2,1,0:T(8,128)(2,1)S(1)}, u32[]{:S(2)}, u32[]{:S(2)}) async-start(bf16[16,1,128,256]{3,2,1,0:T(8,128)(2,1)} %bitcast.7), calls=%async_computation.1 | async-start | bytes 2097152 | tf_op jit(solution)/shard_map/all_to_all | solution.py:89
  62.4 5.2 %copy-start.1 = (s32[1,16,1]{1,2,0:T(1,128)S(1)}, s32[1,16,1]{1,2,0:T(1,128)}, u32[]{:S(2)}) copy-start(s32[1,16,1]{1,2,0:T(1,128)} %param.9) | copy-start | bytes 196
  62.4 31.0 %all-to-all-start.2 = ((f32[8,16,32,128]{3,2,1,0:T(8,128)}), f32[8,16,32,128]{3,2,1,0:T(8,128)S(1)}, u32[]{:S(2)}, u32[]{:S(2)}) async-start(f32[8,16,32,128]{3,2,1,0:T(8,128)} %shard_map.64), calls=%async_computation.2 | async-start | bytes 4194304 | tf_op jit(solution)/shard_map/all_to_all | solution.py:94
  95.0 16.9 %all-to-all-start.3 = ((f32[16,2,32,128]{3,2,1,0:T(8,128)}), f32[16,2,32,128]{3,2,1,0:T(8,128)S(1)}, u32[]{:S(2)}, u32[]{:S(2)}) async-start(f32[16,2,32,128]{3,2,1,0:T(8,128)} %bitcast.13), calls=%async_computation.3 | async-start | bytes 1048576 | tf_op jit(solution)/shard_map/all_to_all | solution.py:112

commit v10 on v5

--- a/solution.py
+++ b/solution.py
@@ -8,7 +8,7 @@
 from jax.sharding import PartitionSpec as P
 
 CAP = 2
-P_CHUNK = 4
+P_CHUNK = 8
 ROW_CHUNK = 512
 
 

time: 113 us -> 113 us (level)
  no operation moved by 1% of the time
where the time goes in v10:
time: 113 us
  waiting for transfers between devices  46.1 us (41%)
  Pallas kernels  22.6 us (20%)
  blocking collectives  15.2 us (13%)
  starting transfers between devices  15.1 us (13%)
  local copies, waits for them, and re-layouts  9.94 us (9%)
  other arithmetic  3.93 us (3%)
    all_to_all x1, waiting for transfers between devices, local(): reduced = jnp.sum(lax.all_to_all(partial, 'aux', 0, 0, tiled=True), axis=0)  25.2 us
    pallas_call x1, Pallas kernels, tile_partials(): pl.pallas_call(tile_kernel, grid=(n_p // P_CHUNK,), in_specs=[pl.BlockSpe...  22.6 us
    all_to_all x1, blocking collectives, local(): ints_got = lax.all_to_all(ints, 'blk', 0, 0, tiled=True)  15.2 us
    all_to_all x1, waiting for transfers between devices, local(): lax.all_to_all(send_panels, 'blk', 0, 0, tiled=True).reshape(tiles, bs, occ)  10.8 us
    all_to_all x1, waiting for transfers between devices, local(): received = lax.all_to_all(send_tiles, 'blk', 0, 0, tiled=True)  10.1 us
    transpose x1, local copies, waits for them, and re-layouts, local(): slab_t = jnp.swapaxes(slab_factor, 1, 2).reshape(n_p * occ, slab)  6.42 us
    all_to_all x1, starting transfers between devices, local(): received = lax.all_to_all(send_tiles, 'blk', 0, 0, tiled=True)  5.75 us
    all_to_all x1, starting transfers between devices, local(): reduced = jnp.sum(lax.all_to_all(partial, 'aux', 0, 0, tiled=True), axis=0)  5.23 us
  transfers between devices with their start and end apart: 3, of which 3 were waited for; matrix products, arithmetic and copies ran while one was open for 7% of the time, Pallas kernels for 0%

profile of v10, /device:TPU:1, one launch (start us, length us, event | category | flops | bytes accessed | tf_op | source)
XLA Modules:
  0.0 112.9 jit_solution(10162409871199519763)
XLA Ops:
  0.0 0.0 copy-start
  0.0 0.8 copy.21
  0.8 0.7 pad_add_fusion.1
  1.5 0.1 pad.5.clone
  1.6 15.2 %all_to_all.27 = s32[16,1,33]{2,1,0:T(1,128)S(1)} all-to-all(s32[16,1,33]{2,1,0:T(1,128)S(1)} %bitcast.33), channel_id=1, replica_groups=mesh['blk'=16,'aux'=8] {'blk'}, dimensions={0} | all-to-all | bytes 4224 | tf_op jit(solution)/shard_map/all_to_all | solution.py:82
  16.8 0.1 fusion.1
  17.0 0.0 copy-done
  17.0 1.6 %gather_fusion = bf16[16,128,256]{2,1,0:T(8,128)(2,1)} fusion(bf16[4,128,256]{2,1,0:T(8,128)(2,1)S(1)} %bitcast.21, s32[1024]{0:T(1024)S(1)} %pad_clamp_fusion.1), kind=kCustom, calls=%fused_computation | custom fusion | bytes 2097216 | tf_op jit(solution)/shard_map/gather | solution.py:88
  18.6 4.1 %all-to-all-start.1 = ((bf16[16,1,128,256]{3,2,1,0:T(8,128)(2,1)}), bf16[16,1,128,256]{3,2,1,0:T(8,128)(2,1)S(1)}, u32[]{:S(2)}, u32[]{:S(2)}) async-start(bf16[16,1,128,256]{3,2,1,0:T(8,128)(2,1)} %bitcast.7), calls=%async_computation.1 | async-start | bytes 2097152 | tf_op jit(solution)/shard_map/all_to_all | solution.py:89
  22.7 6.4 %copy.23 = bf16[32,256,256]{2,1,0:T(8,128)(2,1)} copy(bf16[32,256,256]{1,2,0:T(8,128)(2,1)} %bitcast.23) | data formatting | bytes 8388608 | tf_op jit(solution)/shard_map/transpose | solution.py:92
  29.1 10.8 %all-to-all-done.1 = bf16[16,1,128,256]{3,2,1,0:T(8,128)(2,1)S(1)} async-done(((bf16[16,1,128,256]{3,2,1,0:T(8,128)(2,1)}), bf16[16,1,128,256]{3,2,1,0:T(8,128)(2,1)S(1)}, u32[]{:S(2)}, u32[]{:S(2)}) %all-to-all-start.1) | async-done | bytes 1048608 | tf_op jit(solution)/shard_map/all_to_all | solution.py:89
  39.8 22.6 %shard_map.64 = f32[8,16,32,128]{3,2,1,0:T(8,128)} custom-call(bf16[16,32,128,128]{3,2,1,0:T(8,128)(2,1)} %bitcast.35, bf16[16,128,256]{2,1,0:T(8,128)(2,1)S(1)} %bitcast.22, bf16[8192,256]{1,0:T(8,128)(2,1)} %bitcast.24), custom_call_target="tpu_custom_call" | custom-call | flops 12884901888 | bytes 24117248 | tf_op jit(solution)/shard_map/pallas_call | solution.py:47
  62.4 0.0 copy-start.1
  62.4 5.2 %all-to-all-start.2 = ((f32[8,16,32,128]{3,2,1,0:T(8,128)}), f32[8,16,32,128]{3,2,1,0:T(8,128)S(1)}, u32[]{:S(2)}, u32[]{:S(2)}) async-start(f32[8,16,32,128]{3,2,1,0:T(8,128)} %shard_map.64), calls=%async_computation.2 | async-start | bytes 4194304 | tf_op jit(solution)/shard_map/all_to_all | solution.py:94
  67.7 0.0 copy-done.1
  67.7 0.2 convert_reduce_fusion.1
  67.9 0.1 fusion.2
  68.0 0.1 broadcast_in_dim.91
  68.1 0.1 select_reduce_fusion.5
  68.2 0.1 fusion.4
  68.3 25.2 %all-to-all-done.2 = f32[8,16,32,128]{3,2,1,0:T(8,128)S(1)} async-done(((f32[8,16,32,128]{3,2,1,0:T(8,128)}), f32[8,16,32,128]{3,2,1,0:T(8,128)S(1)}, u32[]{:S(2)}, u32[]{:S(2)}) %all-to-all-start.2) | async-done | bytes 2097184 | tf_op jit(solution)/shard_map/all_to_all | solution.py:94
  93.5 0.2 reduce_sum.86
  93.7 0.6 gather_fusion.1
  94.3 0.9 broadcast_select_fusion
  95.2 5.8 %all-to-all-start.3 = ((f32[16,2,32,128]{3,2,1,0:T(8,128)}), f32[16,2,32,128]{3,2,1,0:T(8,128)S(1)}, u32[]{:S(2)}, u32[]{:S(2)}) async-start(f32[16,2,32,128]{3,2,1,0:T(8,128)} %broadcast_select_fusion), calls=%async_computation.3 | async-start | bytes 1048576 | tf_op jit(solution)/shard_map/all_to_all | solution.py:112
  100.9 0.1 broadcast_compare_fusion
  101.0 0.4 convert_reduce_fusion
  101.4 0.1 select_reduce_fusion.4
  101.6 0.1 copy.22
  101.7 0.1 copy.24
  101.8 0.1 copy.25
  101.9 0.1 copy.26
  102.0 10.1 %all-to-all-done.3 = f32[16,2,32,128]{3,2,1,0:T(8,128)S(1)} async-done(((f32[16,2,32,128]{3,2,1,0:T(8,128)}), f32[16,2,32,128]{3,2,1,0:T(8,128)S(1)}, u32[]{:S(2)}, u32[]{:S(2)}) %all-to-all-start.3) | async-done | bytes 524320 | tf_op jit(solution)/shard_map/all_to_all | solution.py:112
  112.1 0.2 select_reduce_fusion.3
  112.3 0.6 pad_maximum_fusion
  (7 shorter events, 0.1 us)
Async XLA Ops:
  0.0 17.0 %copy-start = (bf16[512,256]{1,0:T(8,128)(2,1)S(1)}, bf16[512,256]{1,0:T(8,128)(2,1)}, u32[]{:S(2)}) copy-start(bf16[512,256]{1,0:T(8,128)(2,1)} %param.8) | copy-start | bytes 786436
  18.6 21.3 %all-to-all-start.1 = ((bf16[16,1,128,256]{3,2,1,0:T(8,128)(2,1)}), bf16[16,1,128,256]{3,2,1,0:T(8,128)(2,1)S(1)}, u32[]{:S(2)}, u32[]{:S(2)}) async-start(bf16[16,1,128,256]{3,2,1,0:T(8,128)(2,1)} %bitcast.7), calls=%async_computation.1 | async-start | bytes 2097152 | tf_op jit(solution)/shard_map/all_to_all | solution.py:89
  62.4 5.2 %copy-start.1 = (s32[1,16,1]{1,2,0:T(1,128)S(1)}, s32[1,16,1]{1,2,0:T(1,128)}, u32[]{:S(2)}) copy-start(s32[1,16,1]{1,2,0:T(1,128)} %param.9) | copy-start | bytes 196
  62.4 31.0 %all-to-all-start.2 = ((f32[8,16,32,128]{3,2,1,0:T(8,128)}), f32[8,16,32,128]{3,2,1,0:T(8,128)S(1)}, u32[]{:S(2)}, u32[]{:S(2)}) async-start(f32[8,16,32,128]{3,2,1,0:T(8,128)} %shard_map.64), calls=%async_computation.2 | async-start | bytes 4194304 | tf_op jit(solution)/shard_map/all_to_all | solution.py:94
  95.2 16.9 %all-to-all-start.3 = ((f32[16,2,32,128]{3,2,1,0:T(8,128)}), f32[16,2,32,128]{3,2,1,0:T(8,128)S(1)}, u32[]{:S(2)}, u32[]{:S(2)}) async-start(f32[16,2,32,128]{3,2,1,0:T(8,128)} %broadcast_select_fusion), calls=%async_computation.3 | async-start | bytes 1048576 | tf_op jit(solution)/shard_map/all_to_all | solution.py:112
